TPU v7x, 128 devices: a whole 4x4x4 slice. The times are simulated.
128 devices in a mesh: seq: 32 (over z, x, y_lo), tp: 4 (over y_hi, core).
Axes of the slice: x: 4, y: 4 (y_hi: 2, y_lo: 2; y = y_hi * 2 + y_lo), z: 4, core: 2. Of those that a mesh axis runs over, the one named last changes fastest.
Arguments:
- query_gate: bfloat16 [256, 131072], P('tp', 'seq'), may hold values from -6 to 6
- key_gate: bfloat16 [256, 131072], P('tp', 'seq'), may hold values from -6 to 6
- value_input: bfloat16 [256, 131072], P('tp', 'seq'), may hold values from -6 to 6
- long_filter: float32 [256, 131072], P('tp', 'seq'), may hold values from -2 to 2, as said below
- out_weight: bfloat16 [256, 256], replicated, may hold values from -0.375 to 0.375
Outputs:
- mixed: bfloat16 [256, 131072], P('tp', 'seq')
Inputs may be any that keep to these rules, and one draw needn't show every extreme that they name: `long_filter`: each channel's taps follow a decaying envelope.
All inputs are finite; a program needn't handle non-finite values.
Results may differ from a plain program's by a relative error of at most 0.018.
Values may be sent and summed in bfloat16 or wider, within the bound.
No kernel may reach another device: no remote copies, remote signals or barrier semaphores. Data moves between devices by JAX's collectives and lax.ppermute only.
A program may use at most 64 MiB of HBM per device.

v0:
```python
import math

import jax
import numpy as np
import jax.numpy as jnp
from jax import lax
from jax.experimental import pallas as pl
from jax.sharding import PartitionSpec as P

HIGH = lax.Precision.HIGH


def turn_table(row_ids, col_ids, modulus):
    turns = (np.asarray(row_ids, np.int64)[:, None] * np.asarray(col_ids, np.int64)[None, :]) % modulus
    angles = turns.astype(np.float64) * (2.0 * math.pi / modulus)
    return (jnp.asarray(np.cos(angles), jnp.float32), jnp.asarray(np.sin(angles), jnp.float32))


def block_table(cos, sin, sign, cols_reim_inner, rows_reim_inner=False):
    n_out, n_in = cos.shape
    tab = np.zeros((2, n_out, 2, n_in))
    tab[0, :, 0], tab[0, :, 1] = cos, -sign * sin
    tab[1, :, 0], tab[1, :, 1] = sign * sin, cos
    if cols_reim_inner:
        tab = tab.transpose(0, 1, 3, 2)
    if rows_reim_inner:
        tab = tab.transpose(1, 0, 2, 3)
    return jnp.asarray(tab.reshape(2 * n_out, 2 * n_in), jnp.float32)


def np_turns(row_ids, col_ids, modulus):
    turns = (np.asarray(row_ids, np.int64)[:, None] * np.asarray(col_ids, np.int64)[None, :]) % modulus
    angles = turns.astype(np.float64) * (2.0 * math.pi / modulus)
    return np.cos(angles), np.sin(angles)


def row_list(seqs):
    return np.array([d if s == 0 else (seqs if d == 0 else 2 * seqs - d) for d in range(seqs) for s in range(2)])


def slot_rows(device, slot, seqs):
    return jnp.where(slot == 0, device, jnp.where(device == 0, seqs, 2 * seqs - device))


def major(table, data):
    return jnp.einsum("qk,k...->q...", table, data, precision=HIGH)


def minor(data, table):
    return jnp.einsum("...b,bm->...m", data, table, precision=HIGH)


def send_blocks(key_gate, value_input, long_filter, seqs, interpret=False):
    chans, length = key_gate.shape
    width = length // seqs
    pairs = chans // 2

    def kernel(key_ref, value_ref, taps_ref, out_ref):
        for d in range(seqs):
            cols = slice(d * width, (d + 1) * width)
            gated = key_ref[:, cols].astype(jnp.float32) * value_ref[:, cols].astype(jnp.float32)
            gated = gated.astype(jnp.bfloat16)
            taps = taps_ref[:, cols].astype(jnp.bfloat16)
            out_ref[d, 0:pairs] = gated[:pairs]
            out_ref[d, pairs:chans] = taps[:pairs]
            out_ref[d, chans:chans + pairs] = gated[pairs:]
            out_ref[d, chans + pairs:2 * chans] = taps[pairs:]

    return pl.pallas_call(
        kernel,
        out_shape=jax.ShapeDtypeStruct((seqs, 2 * chans, width), jnp.bfloat16),
        interpret=interpret,
    )(key_gate, value_input, long_filter)


def body(query_gate, key_gate, value_input, long_filter, out_weight):
    chans, length = key_gate.shape
    seqs = lax.axis_size("seq")
    seq_index = lax.axis_index("seq")
    width = length // seqs
    rows = 2 * seqs
    full = rows * length
    pairs = chans // 2
    f32, bf16 = jnp.float32, jnp.bfloat16

    send = send_blocks(key_gate, value_input, long_filter, seqs)
    got = lax.all_to_all(send, "seq", 0, 0, tiled=True).astype(f32)
    packed_real, packed_imag = got[:, :chans], got[:, chans:]

    row_ids = row_list(seqs)
    cos_a, sin_a = turn_table(row_ids, np.arange(seqs), rows)
    freq_real = major(cos_a, packed_real) + major(sin_a, packed_imag)
    freq_imag = major(cos_a, packed_imag) - major(sin_a, packed_real)
    cos_dev, sin_dev = turn_table(np.arange(seqs) * width, row_ids, full)
    cos_dev = lax.dynamic_index_in_dim(cos_dev, seq_index, 0, keepdims=False)[:, None, None]
    sin_dev = lax.dynamic_index_in_dim(sin_dev, seq_index, 0, keepdims=False)[:, None, None]
    cos_col, sin_col = turn_table(row_ids, np.arange(width), full)
    cos_col, sin_col = cos_col[:, None, :], sin_col[:, None, :]
    cos_t = cos_dev * cos_col - sin_dev * sin_col
    sin_t = sin_dev * cos_col + cos_dev * sin_col
    spread_real = freq_real * cos_t + freq_imag * sin_t
    spread_imag = freq_imag * cos_t - freq_real * sin_t
    spread = jnp.stack([spread_real, spread_imag], axis=1).astype(bf16)
    spread = spread.reshape(seqs, 2, 2, chans, width).transpose(0, 2, 1, 3, 4)
    recv = lax.all_to_all(spread, "seq", 0, 0, tiled=True).astype(f32)

    cos_o, sin_o = turn_table(np.arange(seqs), np.arange(seqs), seqs)
    cos_w, sin_w = turn_table(np.arange(seqs), np.arange(width), length)
    cos_w, sin_w = cos_w[:, None, None, :], sin_w[:, None, None, :]
    cos_i, sin_i = turn_table(np.arange(width), np.arange(width), width)
    co_np, so_np = np_turns(np.arange(seqs), np.arange(seqs), seqs)
    first = major(block_table(co_np, so_np, -1.0, True), recv.reshape((2 * seqs,) + recv.shape[2:]))
    first_real, first_imag = first[:seqs], first[seqs:]
    twist_real = first_real * cos_w + first_imag * sin_w
    twist_imag = first_imag * cos_w - first_real * sin_w
    fwd_block = jnp.concatenate(
        [jnp.concatenate([cos_i, -sin_i], axis=1), jnp.concatenate([sin_i, cos_i], axis=1)], axis=0
    )
    inv_block = jnp.concatenate(
        [jnp.concatenate([cos_i, sin_i], axis=1), jnp.concatenate([-sin_i, cos_i], axis=1)], axis=0
    )
    spec = minor(jnp.concatenate([twist_real, twist_imag], axis=-1), fwd_block)
    spec_real, spec_imag = spec[..., :width], spec[..., width:]

    lane_in = lax.broadcasted_iota(jnp.int32, (width, width), 0)
    lane_out = lax.broadcasted_iota(jnp.int32, (width, width), 1)
    lane_flip = (lane_in == width - 1 - lane_out).astype(f32)
    lane_neg = (lane_in == (width - lane_out) % width).astype(f32)
    place = lax.broadcasted_iota(jnp.int32, (rows, rows), 0)
    source = lax.broadcasted_iota(jnp.int32, (rows, rows), 1)
    place_q, place_s = place // 2, place % 2
    cross_src = 2 * (seqs - 1 - place_q) + 1 - place_s
    self_src = jnp.where(place_s == 1, 2 * (seqs - 1 - place_q) + 1, 2 * ((seqs - place_q) % seqs))
    first_dev = seq_index == 0
    regroup = (source == jnp.where(first_dev, self_src, cross_src)).astype(f32)

    def negated(spec):
        flipped = jnp.einsum("...b,bm->...m", spec, lane_flip, precision=HIGH)
        moved = jnp.einsum(
            "uv,vcb->ucb", regroup, flipped.reshape(rows, chans, width), precision=HIGH
        ).reshape(spec.shape)
        corner = jnp.einsum("cb,bm->cm", spec[0, 0], lane_neg, precision=HIGH)
        return moved.at[0, 0].set(jnp.where(first_dev, corner, moved[0, 0]))

    neg_real = negated(spec_real)
    neg_imag = negated(spec_imag)

    a_real = 0.5 * (spec_real + neg_real)
    a_imag = 0.5 * (spec_imag - neg_imag)
    b_real = 0.5 * (spec_imag + neg_imag)
    b_imag = 0.5 * (neg_real - spec_real)
    sig1_r, sig1_i, filt1_r, filt1_i = (
        a_real[:, :, :pairs], a_imag[:, :, :pairs], a_real[:, :, pairs:], a_imag[:, :, pairs:]
    )
    sig2_r, sig2_i, filt2_r, filt2_i = (
        b_real[:, :, :pairs], b_imag[:, :, :pairs], b_real[:, :, pairs:], b_imag[:, :, pairs:]
    )
    prod1_r = sig1_r * filt1_r - sig1_i * filt1_i
    prod1_i = sig1_r * filt1_i + sig1_i * filt1_r
    prod2_r = sig2_r * filt2_r - sig2_i * filt2_i
    prod2_i = sig2_r * filt2_i + sig2_i * filt2_r
    prod_real = prod1_r - prod2_i
    prod_imag = prod1_i + prod2_r

    inv = minor(jnp.concatenate([prod_real, prod_imag], axis=-1), inv_block)
    inv_real, inv_imag = inv[..., :width], inv[..., width:]
    untwist_real = inv_real * cos_w - inv_imag * sin_w
    untwist_imag = inv_imag * cos_w + inv_real * sin_w
    untwist = jnp.stack([untwist_real, untwist_imag], axis=0)
    back = major(block_table(co_np, so_np, 1.0, False), untwist.reshape((2 * seqs,) + untwist.shape[2:]))
    back_real, back_imag = back[:seqs], back[seqs:]

    own_rows = slot_rows(seq_index, jnp.arange(2), seqs)
    cos_blk, sin_blk = turn_table(np.arange(rows), np.arange(seqs) * width, full)
    cos_off, sin_off = turn_table(np.arange(rows), np.arange(width), full)
    cos_blk, sin_blk = jnp.take(cos_blk, own_rows, axis=0).T, jnp.take(sin_blk, own_rows, axis=0).T
    cos_off, sin_off = jnp.take(cos_off, own_rows, axis=0), jnp.take(sin_off, own_rows, axis=0)
    cos_b = (cos_blk[:, :, None] * cos_off[None] - sin_blk[:, :, None] * sin_off[None])[:, :, None, :]
    sin_b = (sin_blk[:, :, None] * cos_off[None] + cos_blk[:, :, None] * sin_off[None])[:, :, None, :]
    reverted_real = back_real * cos_b - back_imag * sin_b
    reverted_imag = back_imag * cos_b + back_real * sin_b
    reverted = jnp.stack([reverted_real, reverted_imag], axis=2).astype(bf16)
    moved = lax.all_to_all(reverted, "seq", 0, 0, tiled=True).astype(f32)
    moved = moved.reshape(2 * rows, pairs, width)

    cl_np, sl_np = np_turns(np.arange(seqs), row_ids, rows)
    merged = major(block_table(cl_np, sl_np, 1.0, True, rows_reim_inner=True), moved)
    merged = merged.reshape(seqs, chans, width) * (1.0 / full)
    arrived = lax.all_to_all(merged.astype(bf16), "seq", 0, 0, tiled=True)
    conv = arrived.astype(f32).transpose(1, 0, 2).reshape(chans, length)
    gated_out = (query_gate.astype(f32) * conv).astype(bf16)

    tp_index = lax.axis_index("tp")
    tps = lax.axis_size("tp")
    other_chip = tp_index ^ 2
    other_core = tp_index ^ 1
    cross = [(i, i ^ 2) for i in range(tps)]
    gated_far = lax.ppermute(gated_out, "tp", cross)

    def weights(rows_of, cols_of):
        return lax.dynamic_slice(out_weight, (rows_of * chans, cols_of * chans), (chans, chans))

    def partial(rows_of):
        near = jnp.dot(weights(rows_of, tp_index), gated_out, preferred_element_type=f32)
        far = jnp.dot(weights(rows_of, other_chip), gated_far, preferred_element_type=f32)
        return near + far

    pair = [(i, i ^ 1) for i in range(tps)]
    send_part = partial(other_core)
    keep_part = partial(tp_index)
    total = keep_part + lax.ppermute(send_part.astype(bf16), "tp", pair).astype(f32)
    return total.astype(bf16)


def solution(mesh):
    return jax.shard_map(
        body,
        mesh=mesh,
        in_specs=(P("tp", "seq"), P("tp", "seq"), P("tp", "seq"), P("tp", "seq"), P()),
        out_specs=P("tp", "seq"),
        check_vma=False,
    )
```

profile of v0, /device:TPU:1, one launch (start us, length us, event | category | flops | bytes accessed | tf_op | source)
XLA Modules:
  0.0 151.7 jit_solution(11562639341404999340)
XLA Ops:
  0.0 2.7 %shard_map.208 = bf16[32,128,128]{2,1,0:T(8,128)(2,1)} custom-call(bf16[64,4096]{1,0:T(8,128)(2,1)} %key_ref.1, bf16[64,4096]{1,0:T(8,128)(2,1)} %value_ref.1, f32[64,4096]{1,0:T(8,128)} %taps_ref.1), custom_call_target="tpu_custom_call" | custom-call | tf_op jit(solution)/shard_map/pallas_call | solution.py:69
  2.7 9.8 %all-to-all-start = ((bf16[32,128,128]{2,1,0:T(8,128)(2,1)}), bf16[32,128,128]{2,1,0:T(8,128)(2,1)S(1)}, u32[]{:S(2)}, u32[]{:S(2)}) async-start(bf16[32,128,128]{2,1,0:T(8,128)(2,1)} %shard_map.208), calls=%async_computation | async-start | bytes 2097152 | tf_op jit(solution)/shard_map/all_to_all | solution.py:87
  12.6 0.7 fusion.68
  13.3 0.1 multiply_subtract_fusion.2
  13.4 15.9 %all-to-all-done = bf16[32,128,128]{2,1,0:T(8,128)(2,1)S(1)} async-done(((bf16[32,128,128]{2,1,0:T(8,128)(2,1)}), bf16[32,128,128]{2,1,0:T(8,128)(2,1)S(1)}, u32[]{:S(2)}, u32[]{:S(2)}) %all-to-all-start) | async-done | bytes 1048608 | tf_op jit(solution)/shard_map/all_to_all | solution.py:87
  29.3 0.1 fusion.72
  29.3 0.0 copy-start.6
  29.4 0.8 fusion.39
  30.1 0.8 fusion.35
  30.9 0.9 convolution_add_fusion.2
  31.9 1.4 fusion.14
  33.3 3.4 %copy_bitcast_fusion = bf16[32,2,2,64,128]{4,2,3,1,0:T(2,128)(2,1)} fusion(bf16[32,2,1,64,128]{4,1,0,3,2:T(2,128)(2,1)S(1)} %bitcast.121, bf16[32,2,1,64,128]{4,1,0,3,2:T(2,128)(2,1)S(1)} %bitcast.120), kind=kLoop, calls=%fused_computation.22 | loop fusion | flops 1048576 | bytes 4194304 | tf_op jit(solution)/shard_map/transpose | solution.py:104
  36.7 4.2 %all-to-all-start.1 = ((bf16[32,2,2,64,128]{4,2,3,1,0:T(2,128)(2,1)}), bf16[32,2,2,64,128]{4,2,3,1,0:T(2,128)(2,1)S(1)}, u32[]{:S(2)}, u32[]{:S(2)}) async-start(bf16[32,2,2,64,128]{4,2,3,1,0:T(2,128)(2,1)} %copy_bitcast_fusion), calls=%async_computation.1 | async-start | bytes 4194304 | tf_op jit(solution)/shard_map/all_to_all | solution.py:105
  41.0 0.1 fusion.46
  41.2 1.3 gather_fusion
  42.5 1.3 gather_fusion.2
  43.8 1.3 gather_fusion.1
  45.1 1.3 gather_fusion.3
  46.5 0.1 select_bitcast_fusion.1
  46.5 0.1 broadcast_select_fusion.1
  46.6 0.1 multiply_subtract_fusion.1
  46.7 0.0 copy-start.9
  46.7 21.7 %all-to-all-done.1 = bf16[32,2,2,64,128]{4,2,3,1,0:T(2,128)(2,1)S(1)} async-done(((bf16[32,2,2,64,128]{4,2,3,1,0:T(2,128)(2,1)}), bf16[32,2,2,64,128]{4,2,3,1,0:T(2,128)(2,1)S(1)}, u32[]{:S(2)}, u32[]{:S(2)}) %all-to-all-start.1) | async-done | bytes 2097184 | tf_op jit(solution)/shard_map/all_to_all | solution.py:105
  68.4 2.2 %copy.79 = bf16[32,2,2,64,128]{4,1,0,3,2:T(2,128)(2,1)S(1)} copy(bf16[32,2,2,64,128]{4,2,3,1,0:T(2,128)(2,1)S(1)} %all-to-all-done.1) | data formatting | bytes 4194304 | tf_op jit(solution)/shard_map/all_to_all | solution.py:105
  70.6 0.0 copy-start.4
  70.6 0.0 copy-start.5
  70.6 1.2 fusion.73
  71.9 0.6 multiply_add_fusion
  72.5 0.0 copy-start.3
  72.5 0.4 pad_maximum_fusion
  72.9 0.5 copy-done.3
  73.4 3.9 %fusion.3 = f32[32,2,64,256]{3,2,1,0:T(8,128)S(1)} fusion(f32[256,256,1,1]{1,0,3,2:T(8,128)S(1)} %copy-done.3, f32[32,2,64,256]{3,0,2,1:T(8,128)S(1)} %pad_maximum_fusion), kind=kOutput, calls=%fused_computation.10 | convolution fusion | flops 1610612736 | bytes 8650752 | tf_op jit(solution)/shard_map/...b,bm->...m/dot_general | solution.py:50
  77.4 0.7 fusion.21
  78.1 0.7 fusion.23
  78.8 2.2 %fusion.9 = f32[32,2,64,128]{3,0,2,1:T(8,128)S(1)} fusion(f32[64,64,128]{2,1,0:T(8,128)S(1)} %bitcast.118, pred[32,2,64,1]{2,1,0,3:T(4,128)(4,1)S(1)} %bitcast.123), kind=kOutput, calls=%fused_computation.18 | convolution fusion | flops 201326592 | bytes 4198400 | tf_op jit(solution)/shard_map/uv,vcb->ucb/dot_general | solution.py:139
  81.0 1.2 copy.88
  82.3 2.0 %fusion.11 = f32[32,2,64,128]{3,0,2,1:T(8,128)S(1)} fusion(f32[64,64,128]{2,1,0:T(8,128)S(1)} %bitcast.116, pred[32,2,64,1]{2,1,0,3:T(4,128)(4,1)S(1)} %bitcast.124), kind=kOutput, calls=%fused_computation.20 | convolution fusion | flops 201326592 | bytes 4198400 | tf_op jit(solution)/shard_map/uv,vcb->ucb/dot_general | solution.py:139
  84.2 1.2 copy.84
  85.5 0.1 fusion.28
  85.6 0.1 fusion.30
  85.8 1.6 %add_multiply_fusion.1 = (f32[32,2,64,128]{3,2,1,0:T(8,128)S(1)}, f32[32,2,64,128]{3,2,1,0:T(8,128)S(1)}, f32[32,2,64,128]{3,2,1,0:T(8,128)S(1)}, f32[32,2,64,128]{3,2,1,0:T(8,128)S(1)}) fusion(f32[32,2,64,128]{3,2,1,0:T(8,128)S(1)} %fusion.30, f32[32,2,64,256]{3,2,1,0:T(8,128)S(1)} %fusion.3, f32[32,2,64,128]{3,2,1,0:T(8,128)S(1)} %fusion.28), kind=kLoop, calls=%fused_computation.38 | loop fusion | flops 4194304 | bytes 16777216 | tf_op jit(solution)/shard_map/mul | solution.py:148
  87.4 1.1 add_subtract_fusion
  88.4 1.0 fusion.5
  89.5 0.3 subtract_bitcast_fusion
  89.8 0.3 pad_maximum_fusion.2
  90.1 0.4 copy-done.8
  90.6 2.2 %fusion.17 = f32[64,2,32,128]{3,0,2,1:T(8,128)S(1)} fusion(f32[64,64,1,1]{1,0,3,2:T(8,128)S(1)} %copy-done.8, f32[64,2,32,128]{3,2,1,0:T(8,128)S(1)} %bitcast.117), kind=kOutput, calls=%fused_computation.31 | convolution fusion | flops 201326592 | bytes 4210688 | tf_op jit(solution)/shard_map/qk,k...->q.../dot_general | solution.py:46
  92.8 0.3 fusion.33
  93.0 0.1 pad_maximum_fusion.3
  93.1 0.4 copy.90
  93.6 23.7 %all_to_all.20 = bf16[32,2,2,32,128]{4,3,1,2,0:T(8,128)(2,1)S(1)} all-to-all(bf16[32,2,2,32,128]{4,3,1,2,0:T(8,128)(2,1)S(1)} %copy.90), channel_id=1, replica_groups=mesh['seq'=32,'tp'=4] {'seq'}, dimensions={0} | all-to-all | bytes 2097152 | tf_op jit(solution)/shard_map/all_to_all | solution.py:183
  117.3 0.1 copy.91
  117.4 0.7 fusion.26
  118.2 0.3 copy.93
  118.5 14.1 %all_to_all.21 = bf16[32,64,128]{2,1,0:T(8,128)(2,1)S(1)} all-to-all(bf16[32,64,128]{2,1,0:T(8,128)(2,1)S(1)} %bitcast.122), channel_id=1, replica_groups=mesh['seq'=32,'tp'=4] {'seq'}, dimensions={0} | all-to-all | bytes 1048576 | tf_op jit(solution)/shard_map/all_to_all | solution.py:189
  132.6 0.1 fusion.31
  132.7 2.7 %collective-permute-start = (bf16[64,4096]{1,0:T(8,128)(2,1)S(1)}, bf16[64,4096]{1,0:T(8,128)(2,1)S(1)}, u32[]{:S(2)}, u32[]{:S(2)}) collective-permute-start(bf16[64,4096]{1,0:T(8,128)(2,1)S(1)} %fusion.31), channel_id=1, source_target_pairs={{0,2},{1,3},{2,0},{3,1},{4,6},{5,7},{6,4},{7,5},{8,10},{9,11},{10,... | collective-permute-start | bytes 1572872 | tf_op jit(solution)/shard_map/ppermute | solution.py:198
  135.4 0.3 fusion.61
  135.7 9.3 %collective-permute-done = bf16[64,4096]{1,0:T(8,128)(2,1)S(1)} collective-permute-done((bf16[64,4096]{1,0:T(8,128)(2,1)S(1)}, bf16[64,4096]{1,0:T(8,128)(2,1)S(1)}, u32[]{:S(2)}, u32[]{:S(2)}) %collective-permute-start) | collective-permute-done | bytes 524320 | tf_op jit(solution)/shard_map/ppermute | solution.py:198
  145.0 0.3 fusion.2
  145.4 3.7 %collective-permute-start.1 = (bf16[64,4096]{1,0:T(8,128)(2,1)S(1)}, bf16[64,4096]{1,0:T(8,128)(2,1)S(1)}, u32[]{:S(2)}, u32[]{:S(2)}) collective-permute-start(bf16[64,4096]{1,0:T(8,128)(2,1)S(1)} %fusion.2), channel_id=1, source_target_pairs={{0,1},{1,0},{2,3},{3,2},{4,5},{5,4},{6,7},{7,6},{8,9},{9,8},{10,11... | collective-permute-start | bytes 1572872 | tf_op jit(solution)/shard_map/ppermute | solution.py:211
  149.1 0.3 fusion.64
  149.4 1.2 collective-permute-done.1
  150.6 1.1 fusion.1
  (30 shorter events, 0.1 us)
Async XLA Ops:
  0.0 135.4 %copy-start = (bf16[256,256]{1,0:T(8,128)(2,1)S(1)}, bf16[256,256]{1,0:T(8,128)(2,1)}, u32[]{:S(2)}) copy-start(bf16[256,256]{1,0:T(8,128)(2,1)} %param.34) | copy-start | bytes 393220
  0.0 13.3 %copy-start.11 = (f32[64,128]{1,0:T(8,128)S(1)}, f32[64,128]{1,0:T(8,128)}, u32[]{:S(2)}) copy-start(f32[64,128]{1,0:T(8,128)} %constant.193.clone) | copy-start | bytes 98308
  0.0 13.3 %copy-start.12 = (f32[64,128]{1,0:T(8,128)S(1)}, f32[64,128]{1,0:T(8,128)}, u32[]{:S(2)}) copy-start(f32[64,128]{1,0:T(8,128)} %constant.194.clone) | copy-start | bytes 98308
  2.7 26.6 %copy-start.7 = (f32[64,32,1]{0,1,2:T(8,128)S(1)}, f32[64,32,1]{0,1,2:T(8,128)}, u32[]{:S(2)}) copy-start(f32[64,32,1]{0,1,2:T(8,128)} %constant.215) | copy-start | bytes 24580
  2.7 26.5 %all-to-all-start = ((bf16[32,128,128]{2,1,0:T(8,128)(2,1)}), bf16[32,128,128]{2,1,0:T(8,128)(2,1)S(1)}, u32[]{:S(2)}, u32[]{:S(2)}) async-start(bf16[32,128,128]{2,1,0:T(8,128)(2,1)} %shard_map.208), calls=%async_computation | async-start | bytes 2097152 | tf_op jit(solution)/shard_map/all_to_all | solution.py:87
  29.3 1.6 %copy-start.6 = (f32[64,32,1]{0,1,2:T(8,128)S(1)}, f32[64,32,1]{0,1,2:T(8,128)}, u32[]{:S(2)}) copy-start(f32[64,32,1]{0,1,2:T(8,128)} %constant.216) | copy-start | bytes 24580
  36.7 31.7 %all-to-all-start.1 = ((bf16[32,2,2,64,128]{4,2,3,1,0:T(2,128)(2,1)}), bf16[32,2,2,64,128]{4,2,3,1,0:T(2,128)(2,1)S(1)}, u32[]{:S(2)}, u32[]{:S(2)}) async-start(bf16[32,2,2,64,128]{4,2,3,1,0:T(2,128)(2,1)} %copy_bitcast_fusion), calls=%async_computation.1 | async-start | bytes 4194304 | tf_op jit(solution)/shard_map/all_to_all | solution.py:105
  46.7 23.9 %copy-start.9 = (f32[64,64,1,1]{1,0,3,2:T(8,128)S(1)}, f32[64,64,1,1]{1,0,3,2:T(8,128)}, u32[]{:S(2)}) copy-start(f32[64,64,1,1]{1,0,3,2:T(8,128)} %constant.214) | copy-start | bytes 49156
  70.6 1.3 copy-start.4
  70.6 1.3 copy-start.5
  72.5 1.0 copy-start.3
  87.4 1.1 copy-start.2
  89.8 0.8 copy-start.8
  93.6 23.9 %copy-start.10 = (f32[64,128,1]{1,0,2:T(8,128)S(1)}, f32[64,128,1]{1,0,2:T(8,128)}, u32[]{:S(2)}) copy-start(f32[64,128,1]{1,0,2:T(8,128)} %constant.219) | copy-start | bytes 98308
  117.4 15.1 %copy-start.1 = (bf16[64,4096]{1,0:T(8,128)(2,1)S(1)}, bf16[64,4096]{1,0:T(8,128)(2,1)}, u32[]{:S(2)}) copy-start(bf16[64,4096]{1,0:T(8,128)(2,1)} %param.30) | copy-start | bytes 1572868
  132.7 12.3 %collective-permute-start = (bf16[64,4096]{1,0:T(8,128)(2,1)S(1)}, bf16[64,4096]{1,0:T(8,128)(2,1)S(1)}, u32[]{:S(2)}, u32[]{:S(2)}) collective-permute-start(bf16[64,4096]{1,0:T(8,128)(2,1)S(1)} %fusion.31), channel_id=1, source_target_pairs={{0,2},{1,3},{2,0},{3,1},{4,6},{5,7},{6,4},{7,5},{8,10},{9,11},{10,... | collective-permute-start | bytes 1572872 | tf_op jit(solution)/shard_map/ppermute | solution.py:198
  145.4 5.2 %collective-permute-start.1 = (bf16[64,4096]{1,0:T(8,128)(2,1)S(1)}, bf16[64,4096]{1,0:T(8,128)(2,1)S(1)}, u32[]{:S(2)}, u32[]{:S(2)}) collective-permute-start(bf16[64,4096]{1,0:T(8,128)(2,1)S(1)} %fusion.2), channel_id=1, source_target_pairs={{0,1},{1,0},{2,3},{3,2},{4,5},{5,4},{6,7},{7,6},{8,9},{9,8},{10,11... | collective-permute-start | bytes 1572872 | tf_op jit(solution)/shard_map/ppermute | solution.py:211
where the time goes:
time: 153 us; the launch traced here: 152 us
  waiting for transfers between devices  48.1 us (31%)
  blocking collectives  37.8 us (25%)
  matrix products  21 us (14%)
  starting transfers between devices  20.4 us (13%)
  local copies, waits for them, and re-layouts  12.6 us (8%)
  other arithmetic  8.73 us (6%)
  Pallas kernels  2.7 us (2%)
    all_to_all x1, blocking collectives, body(): moved = lax.all_to_all(reverted, 'seq', 0, 0, tiled=True).astype(f32)  23.7 us
    all_to_all x1, waiting for transfers between devices, body(): recv = lax.all_to_all(spread, 'seq', 0, 0, tiled=True).astype(f32)  21.7 us
    all_to_all x1, waiting for transfers between devices, body(): got = lax.all_to_all(send, 'seq', 0, 0, tiled=True).astype(f32)  15.9 us
    all_to_all x1, blocking collectives, body(): arrived = lax.all_to_all(merged.astype(bf16), 'seq', 0, 0, tiled=True)  14.1 us
    all_to_all x1, starting transfers between devices, body(): got = lax.all_to_all(send, 'seq', 0, 0, tiled=True).astype(f32)  9.84 us
    ppermute x1, waiting for transfers between devices, body(): gated_far = lax.ppermute(gated_out, 'tp', cross)  9.32 us
    dot_general x7, matrix products, major(): return jnp.einsum('qk,k...->q...', table, data, precision=HIGH)  8.02 us
    dot_general x2, matrix products, minor(): return jnp.einsum('...b,bm->...m', data, table, precision=HIGH)  4.94 us
  transfers between devices with their start and end apart: 4, of which 4 were waited for; matrix products, arithmetic and copies ran while one was open for 5% of the time, Pallas kernels for 0%

commit v1 on v0

--- a/solution.py
+++ b/solution.py
@@ -85,23 +85,24 @@
 
     send = send_blocks(key_gate, value_input, long_filter, seqs)
     got = lax.all_to_all(send, "seq", 0, 0, tiled=True).astype(f32)
-    packed_real, packed_imag = got[:, :chans], got[:, chans:]
+    got = got.reshape((2 * seqs, chans, width))
 
     row_ids = row_list(seqs)
-    cos_a, sin_a = turn_table(row_ids, np.arange(seqs), rows)
-    freq_real = major(cos_a, packed_real) + major(sin_a, packed_imag)
-    freq_imag = major(cos_a, packed_imag) - major(sin_a, packed_real)
+    ca_np, sa_np = np_turns(row_ids, np.arange(seqs), rows)
+    first_tab = block_table(ca_np, sa_np, -1.0, True).reshape(2, seqs, 2, 2 * seqs)
+    first_tab = first_tab.transpose(1, 0, 2, 3).reshape(2 * rows, 2 * seqs)
+    freq = major(first_tab, got).reshape(seqs, 2, 2, chans, width)
+    freq_real, freq_imag = freq[:, 0], freq[:, 1]
     cos_dev, sin_dev = turn_table(np.arange(seqs) * width, row_ids, full)
-    cos_dev = lax.dynamic_index_in_dim(cos_dev, seq_index, 0, keepdims=False)[:, None, None]
-    sin_dev = lax.dynamic_index_in_dim(sin_dev, seq_index, 0, keepdims=False)[:, None, None]
+    cos_dev = lax.dynamic_index_in_dim(cos_dev, seq_index, 0, keepdims=False).reshape(seqs, 2, 1, 1)
+    sin_dev = lax.dynamic_index_in_dim(sin_dev, seq_index, 0, keepdims=False).reshape(seqs, 2, 1, 1)
     cos_col, sin_col = turn_table(row_ids, np.arange(width), full)
-    cos_col, sin_col = cos_col[:, None, :], sin_col[:, None, :]
+    cos_col, sin_col = cos_col.reshape(seqs, 2, 1, width), sin_col.reshape(seqs, 2, 1, width)
     cos_t = cos_dev * cos_col - sin_dev * sin_col
     sin_t = sin_dev * cos_col + cos_dev * sin_col
     spread_real = freq_real * cos_t + freq_imag * sin_t
     spread_imag = freq_imag * cos_t - freq_real * sin_t
     spread = jnp.stack([spread_real, spread_imag], axis=1).astype(bf16)
-    spread = spread.reshape(seqs, 2, 2, chans, width).transpose(0, 2, 1, 3, 4)
     recv = lax.all_to_all(spread, "seq", 0, 0, tiled=True).astype(f32)
 
     cos_o, sin_o = turn_table(np.arange(seqs), np.arange(seqs), seqs)

time: 153 us -> 155 us (1.013)
  other arithmetic: 8.73 us -> 11.9 us
  local copies, waits for them, and re-layouts: 12.6 us -> 15.5 us
  matrix products: 21 us -> 18.4 us
    another operation x0 -> x2, other arithmetic: none -> 6.53 us  [the longest x1 4.31 us: body(): spread = jnp.stack([spread_real, spread_imag], axis=1).astype(bf16)]
    transpose x1 -> x0, other arithmetic: 3.41 us -> none  [body(): spread = spread.reshape(seqs, 2, 2, chans, width).transpose(0, 2, 1, 3, 4)]
    dot_general x7 -> x4, matrix products: 8.02 us -> 5.62 us  [major(): return jnp.einsum('qk,k...->q...', table, data, precision=HIGH)]
    slice x1, local copies, waits for them, and re-layouts: 0.07 us -> 2.39 us  [body(): freq_real, freq_imag = (freq[:, 0], freq[:, 1])]
where the time goes in v1:
time: 155 us
  waiting for transfers between devices  47.6 us (31%)
  blocking collectives  37.8 us (24%)
  starting transfers between devices  20.3 us (13%)
  matrix products  18.4 us (12%)
  local copies, waits for them, and re-layouts  15.5 us (10%)
  other arithmetic  11.9 us (8%)
  Pallas kernels  2.71 us (2%)
    all_to_all x1, blocking collectives, body(): moved = lax.all_to_all(reverted, 'seq', 0, 0, tiled=True).astype(f32)  23.7 us
    all_to_all x1, waiting for transfers between devices, body(): recv = lax.all_to_all(spread, 'seq', 0, 0, tiled=True).astype(f32)  21.7 us
    all_to_all x1, waiting for transfers between devices, body(): got = lax.all_to_all(send, 'seq', 0, 0, tiled=True).astype(f32)  15.4 us
    all_to_all x1, blocking collectives, body(): arrived = lax.all_to_all(merged.astype(bf16), 'seq', 0, 0, tiled=True)  14.1 us
    all_to_all x1, starting transfers between devices, body(): got = lax.all_to_all(send, 'seq', 0, 0, tiled=True).astype(f32)  9.72 us
    ppermute x1, waiting for transfers between devices, body(): gated_far = lax.ppermute(gated_out, 'tp', cross)  9.28 us
    dot_general x4, matrix products, major(): return jnp.einsum('qk,k...->q...', table, data, precision=HIGH)  5.62 us
    dot_general x2, matrix products, minor(): return jnp.einsum('...b,bm->...m', data, table, precision=HIGH)  4.95 us
  transfers between devices with their start and end apart: 4, of which 4 were waited for; matrix products, arithmetic and copies ran while one was open for 5% of the time, Pallas kernels for 0%

profile of v1, /device:TPU:1, one launch (start us, length us, event | category | flops | bytes accessed | tf_op | source)
XLA Modules:
  0.0 154.5 jit_solution(18097053036540836580)
XLA Ops:
  0.0 0.0 copy-start.8
  0.0 2.7 %shard_map.199 = bf16[32,128,128]{2,1,0:T(8,128)(2,1)} custom-call(bf16[64,4096]{1,0:T(8,128)(2,1)} %key_ref.1, bf16[64,4096]{1,0:T(8,128)(2,1)} %value_ref.1, f32[64,4096]{1,0:T(8,128)} %taps_ref.1), custom_call_target="tpu_custom_call" | custom-call | tf_op jit(solution)/shard_map/pallas_call | solution.py:69
  2.7 9.7 %all-to-all-start = ((bf16[32,128,128]{2,1,0:T(8,128)(2,1)}), bf16[32,128,128]{2,1,0:T(8,128)(2,1)S(1)}, u32[]{:S(2)}, u32[]{:S(2)}) async-start(bf16[32,128,128]{2,1,0:T(8,128)(2,1)} %shard_map.199), calls=%async_computation | async-start | bytes 2097152 | tf_op jit(solution)/shard_map/all_to_all | solution.py:87
  12.5 0.7 fusion.60
  13.2 0.1 mul.325
  13.3 0.1 copy.84
  13.4 0.1 mul.328
  13.5 0.1 copy.85
  13.6 0.1 multiply_subtract_fusion.2
  13.8 15.4 %all-to-all-done = bf16[32,128,128]{2,1,0:T(8,128)(2,1)S(1)} async-done(((bf16[32,128,128]{2,1,0:T(8,128)(2,1)}), bf16[32,128,128]{2,1,0:T(8,128)(2,1)S(1)}, u32[]{:S(2)}, u32[]{:S(2)}) %all-to-all-start) | async-done | bytes 1048608 | tf_op jit(solution)/shard_map/all_to_all | solution.py:87
  29.2 1.5 fusion.29
  30.7 2.4 %fusion.64 = (f32[32,1,2,64,128]{4,2,1,0,3:T(2,128)S(1)}, f32[32,1,2,64,128]{4,2,1,0,3:T(2,128)S(1)}) fusion(f32[32,2,2,64,128]{4,2,1,0,3:T(2,128)S(1)} %bitcast.87), kind=kLoop, calls=%fused_computation.130 | loop fusion | bytes 8388608 | tf_op jit(solution)/shard_map/slice | solution.py:95
  33.1 2.2 %add_convert_fusion = (bf16[32,1,2,64,128]{4,2,1,3,0:T(2,128)(2,1)S(1)}, bf16[32,1,2,64,128]{4,2,1,3,0:T(2,128)(2,1)S(1)}) fusion(f32[32,1,2,64,128]{4,2,1,0,3:T(2,128)S(1)} %get-tuple-element.46, f32[32,1,2,64,128]{4,2,1,0,3:T(2,128)S(1)} %get-tuple-element.45, f32[32,2,128]{2,1,0:T(2,128)S(1)} %copy.88, f32[32,2,128]{2,1,0:T(2,128)S(1)} %copy.86), kind=kLoop, calls=%fused_computation.33 | loop fusion | flops 4194304 | bytes 6356992 | tf_op jit(solution)/shard_map/convert.6
  35.3 4.3 %pad_maximum_fusion.1 = bf16[32,2,2,64,128]{4,2,1,3,0:T(2,128)(2,1)} fusion(bf16[32,1,2,64,128]{4,2,1,3,0:T(2,128)(2,1)S(1)} %get-tuple-element.40, bf16[32,1,2,64,128]{4,2,1,3,0:T(2,128)(2,1)S(1)} %get-tuple-element.39), kind=kLoop, calls=%fused_computation.12 | loop fusion | flops 1048576 | bytes 4194304 | tf_op jit(solution)/shard_map/stack | solution.py:105
  39.6 4.2 %all-to-all-start.1 = ((bf16[32,2,2,64,128]{4,2,1,3,0:T(2,128)(2,1)}), bf16[32,2,2,64,128]{4,2,1,3,0:T(2,128)(2,1)S(1)}, u32[]{:S(2)}, u32[]{:S(2)}) async-start(bf16[32,2,2,64,128]{4,2,1,3,0:T(2,128)(2,1)} %pad_maximum_fusion.1), calls=%async_computation.1 | async-start | bytes 4194304 | tf_op jit(solution)/shard_map/all_to_all | solution.py:106
  43.9 0.1 fusion.38
  44.1 1.3 gather_fusion
  45.4 1.3 gather_fusion.2
  46.7 1.3 gather_fusion.1
  48.0 1.3 gather_fusion.3
  49.4 0.1 select_bitcast_fusion.1
  49.4 0.1 broadcast_select_fusion.1
  49.5 0.1 multiply_subtract_fusion.1
  49.6 0.0 copy-start.7
  49.6 21.7 %all-to-all-done.1 = bf16[32,2,2,64,128]{4,2,1,3,0:T(2,128)(2,1)S(1)} async-done(((bf16[32,2,2,64,128]{4,2,1,3,0:T(2,128)(2,1)}), bf16[32,2,2,64,128]{4,2,1,3,0:T(2,128)(2,1)S(1)}, u32[]{:S(2)}, u32[]{:S(2)}) %all-to-all-start.1) | async-done | bytes 2097184 | tf_op jit(solution)/shard_map/all_to_all | solution.py:106
  71.3 2.1 %copy.89 = bf16[32,2,2,64,128]{4,1,0,3,2:T(2,128)(2,1)S(1)} copy(bf16[32,2,2,64,128]{4,2,1,3,0:T(2,128)(2,1)S(1)} %all-to-all-done.1) | data formatting | bytes 4194304 | tf_op jit(solution)/shard_map/all_to_all | solution.py:106
  73.4 0.0 copy-start.5
  73.5 1.2 fusion.65
  74.7 0.6 multiply_add_fusion
  75.3 0.4 pad_maximum_fusion
  75.8 0.5 copy-done.3
  76.3 3.9 %fusion.3 = f32[32,2,64,256]{3,2,1,0:T(8,128)S(1)} fusion(f32[256,256,1,1]{1,0,3,2:T(8,128)S(1)} %copy-done.3, f32[32,2,64,256]{3,0,2,1:T(8,128)S(1)} %pad_maximum_fusion), kind=kOutput, calls=%fused_computation.10 | convolution fusion | flops 1610612736 | bytes 8650752 | tf_op jit(solution)/shard_map/...b,bm->...m/dot_general | solution.py:50
  80.2 0.7 fusion.17
  80.9 0.7 fusion.19
  81.7 2.0 %fusion.9 = f32[32,2,64,128]{3,0,2,1:T(8,128)S(1)} fusion(f32[64,64,128]{2,1,0:T(8,128)S(1)} %bitcast.91, pred[32,2,64,1]{2,1,0,3:T(4,128)(4,1)S(1)} %bitcast.95), kind=kOutput, calls=%fused_computation.18 | convolution fusion | flops 201326592 | bytes 4198400 | tf_op jit(solution)/shard_map/uv,vcb->ucb/dot_general | solution.py:140
  83.6 1.4 copy.98
  85.1 2.0 %fusion.11 = f32[32,2,64,128]{3,0,2,1:T(8,128)S(1)} fusion(f32[64,64,128]{2,1,0:T(8,128)S(1)} %bitcast.89, pred[32,2,64,1]{2,1,0,3:T(4,128)(4,1)S(1)} %bitcast.96), kind=kOutput, calls=%fused_computation.20 | convolution fusion | flops 201326592 | bytes 4198400 | tf_op jit(solution)/shard_map/uv,vcb->ucb/dot_general | solution.py:140
  87.1 1.2 copy.94
  88.3 0.1 fusion.24
  88.4 0.1 fusion.26
  88.6 1.6 %add_multiply_fusion.1 = (f32[32,2,64,128]{3,2,1,0:T(8,128)S(1)}, f32[32,2,64,128]{3,2,1,0:T(8,128)S(1)}, f32[32,2,64,128]{3,2,1,0:T(8,128)S(1)}, f32[32,2,64,128]{3,2,1,0:T(8,128)S(1)}) fusion(f32[32,2,64,128]{3,2,1,0:T(8,128)S(1)} %fusion.26, f32[32,2,64,256]{3,2,1,0:T(8,128)S(1)} %fusion.3, f32[32,2,64,128]{3,2,1,0:T(8,128)S(1)} %fusion.24), kind=kLoop, calls=%fused_computation.29 | loop fusion | flops 4194304 | bytes 16777216 | tf_op jit(solution)/shard_map/mul | solution.py:149
  90.2 1.1 add_subtract_fusion
  91.3 1.0 fusion.5
  92.3 0.3 subtract_bitcast_fusion
  92.7 0.3 pad_maximum_fusion.2
  93.0 0.4 copy-done.6
  93.4 2.2 %fusion.13 = f32[64,2,32,128]{3,0,2,1:T(8,128)S(1)} fusion(f32[64,64,1,1]{1,0,3,2:T(8,128)S(1)} %copy-done.6, f32[64,2,32,128]{3,2,1,0:T(8,128)S(1)} %bitcast.90), kind=kOutput, calls=%fused_computation.22 | convolution fusion | flops 201326592 | bytes 4210688 | tf_op jit(solution)/shard_map/qk,k...->q.../dot_general | solution.py:46
  95.6 0.3 fusion.31
  95.9 0.1 pad_maximum_fusion.3
  96.0 0.4 copy.100
  96.4 23.7 %all_to_all.20 = bf16[32,2,2,32,128]{4,3,1,2,0:T(8,128)(2,1)S(1)} all-to-all(bf16[32,2,2,32,128]{4,3,1,2,0:T(8,128)(2,1)S(1)} %copy.100), channel_id=1, replica_groups=mesh['seq'=32,'tp'=4] {'seq'}, dimensions={0} | all-to-all | bytes 2097152 | tf_op jit(solution)/shard_map/all_to_all | solution.py:184
  120.1 0.1 copy.101
  120.2 0.7 fusion.22
  121.0 0.3 copy.103
  121.3 14.1 %all_to_all.21 = bf16[32,64,128]{2,1,0:T(8,128)(2,1)S(1)} all-to-all(bf16[32,64,128]{2,1,0:T(8,128)(2,1)S(1)} %bitcast.94), channel_id=1, replica_groups=mesh['seq'=32,'tp'=4] {'seq'}, dimensions={0} | all-to-all | bytes 1048576 | tf_op jit(solution)/shard_map/all_to_all | solution.py:190
  135.4 0.1 fusion.27
  135.5 2.7 %collective-permute-start = (bf16[64,4096]{1,0:T(8,128)(2,1)S(1)}, bf16[64,4096]{1,0:T(8,128)(2,1)S(1)}, u32[]{:S(2)}, u32[]{:S(2)}) collective-permute-start(bf16[64,4096]{1,0:T(8,128)(2,1)S(1)} %fusion.27), channel_id=1, source_target_pairs={{0,2},{1,3},{2,0},{3,1},{4,6},{5,7},{6,4},{7,5},{8,10},{9,11},{10,... | collective-permute-start | bytes 1572872 | tf_op jit(solution)/shard_map/ppermute | solution.py:199
  138.2 0.3 fusion.53
  138.6 9.3 %collective-permute-done = bf16[64,4096]{1,0:T(8,128)(2,1)S(1)} collective-permute-done((bf16[64,4096]{1,0:T(8,128)(2,1)S(1)}, bf16[64,4096]{1,0:T(8,128)(2,1)S(1)}, u32[]{:S(2)}, u32[]{:S(2)}) %collective-permute-start) | collective-permute-done | bytes 524320 | tf_op jit(solution)/shard_map/ppermute | solution.py:199
  147.8 0.4 fusion.2
  148.2 3.6 %collective-permute-start.1 = (bf16[64,4096]{1,0:T(8,128)(2,1)S(1)}, bf16[64,4096]{1,0:T(8,128)(2,1)S(1)}, u32[]{:S(2)}, u32[]{:S(2)}) collective-permute-start(bf16[64,4096]{1,0:T(8,128)(2,1)S(1)} %fusion.2), channel_id=1, source_target_pairs={{0,1},{1,0},{2,3},{3,2},{4,5},{5,4},{6,7},{7,6},{8,9},{9,8},{10,11... | collective-permute-start | bytes 1572872 | tf_op jit(solution)/shard_map/ppermute | solution.py:212
  151.8 0.3 fusion.56
  152.2 1.2 collective-permute-done.1
  153.4 1.1 fusion.1
  (32 shorter events, 0.2 us)
Async XLA Ops:
  0.0 138.2 %copy-start = (bf16[256,256]{1,0:T(8,128)(2,1)S(1)}, bf16[256,256]{1,0:T(8,128)(2,1)}, u32[]{:S(2)}) copy-start(bf16[256,256]{1,0:T(8,128)(2,1)} %param.33) | copy-start | bytes 393220
  0.0 13.6 %copy-start.10 = (f32[32,2,128]{2,0,1:T(8,128)S(1)}, f32[32,2,128]{2,0,1:T(8,128)}, u32[]{:S(2)}) copy-start(f32[32,2,128]{2,0,1:T(8,128)} %constant.206) | copy-start | bytes 98308
  0.0 13.6 %copy-start.11 = (f32[32,2,128]{2,0,1:T(8,128)S(1)}, f32[32,2,128]{2,0,1:T(8,128)}, u32[]{:S(2)}) copy-start(f32[32,2,128]{2,0,1:T(8,128)} %constant.207) | copy-start | bytes 98308
  0.0 29.1 %copy-start.8 = (f32[128,64,1]{0,1,2:T(8,128)S(1)}, f32[128,64,1]{0,1,2:T(8,128)}, u32[]{:S(2)}) copy-start(f32[128,64,1]{0,1,2:T(8,128)} %constant.217) | copy-start | bytes 98308
  2.7 26.4 %all-to-all-start = ((bf16[32,128,128]{2,1,0:T(8,128)(2,1)}), bf16[32,128,128]{2,1,0:T(8,128)(2,1)S(1)}, u32[]{:S(2)}, u32[]{:S(2)}) async-start(bf16[32,128,128]{2,1,0:T(8,128)(2,1)} %shard_map.199), calls=%async_computation | async-start | bytes 2097152 | tf_op jit(solution)/shard_map/all_to_all | solution.py:87
  39.6 31.7 %all-to-all-start.1 = ((bf16[32,2,2,64,128]{4,2,1,3,0:T(2,128)(2,1)}), bf16[32,2,2,64,128]{4,2,1,3,0:T(2,128)(2,1)S(1)}, u32[]{:S(2)}, u32[]{:S(2)}) async-start(bf16[32,2,2,64,128]{4,2,1,3,0:T(2,128)(2,1)} %pad_maximum_fusion.1), calls=%async_computation.1 | async-start | bytes 4194304 | tf_op jit(solution)/shard_map/all_to_all | solution.py:106
  49.6 23.8 %copy-start.7 = (f32[64,64,1,1]{1,0,3,2:T(8,128)S(1)}, f32[64,64,1,1]{1,0,3,2:T(8,128)}, u32[]{:S(2)}) copy-start(f32[64,64,1,1]{1,0,3,2:T(8,128)} %constant.216) | copy-start | bytes 49156
  73.4 1.3 copy-start.4
  73.4 1.3 copy-start.5
  75.3 1.0 copy-start.3
  90.2 1.1 copy-start.2
  92.6 0.8 copy-start.6
  96.4 23.9 %copy-start.9 = (f32[64,128,1]{1,0,2:T(8,128)S(1)}, f32[64,128,1]{1,0,2:T(8,128)}, u32[]{:S(2)}) copy-start(f32[64,128,1]{1,0,2:T(8,128)} %constant.220) | copy-start | bytes 98308
  120.2 15.1 %copy-start.1 = (bf16[64,4096]{1,0:T(8,128)(2,1)S(1)}, bf16[64,4096]{1,0:T(8,128)(2,1)}, u32[]{:S(2)}) copy-start(bf16[64,4096]{1,0:T(8,128)(2,1)} %param.29) | copy-start | bytes 1572868
  135.5 12.3 %collective-permute-start = (bf16[64,4096]{1,0:T(8,128)(2,1)S(1)}, bf16[64,4096]{1,0:T(8,128)(2,1)S(1)}, u32[]{:S(2)}, u32[]{:S(2)}) collective-permute-start(bf16[64,4096]{1,0:T(8,128)(2,1)S(1)} %fusion.27), channel_id=1, source_target_pairs={{0,2},{1,3},{2,0},{3,1},{4,6},{5,7},{6,4},{7,5},{8,10},{9,11},{10,... | collective-permute-start | bytes 1572872 | tf_op jit(solution)/shard_map/ppermute | solution.py:199
  148.2 5.2 %collective-permute-start.1 = (bf16[64,4096]{1,0:T(8,128)(2,1)S(1)}, bf16[64,4096]{1,0:T(8,128)(2,1)S(1)}, u32[]{:S(2)}, u32[]{:S(2)}) collective-permute-start(bf16[64,4096]{1,0:T(8,128)(2,1)S(1)} %fusion.2), channel_id=1, source_target_pairs={{0,1},{1,0},{2,3},{3,2},{4,5},{5,4},{6,7},{7,6},{8,9},{9,8},{10,11... | collective-permute-start | bytes 1572872 | tf_op jit(solution)/shard_map/ppermute | solution.py:212

commit v2 on v0

--- a/solution.py
+++ b/solution.py
@@ -46,6 +46,14 @@
     return jnp.einsum("qk,k...->q...", table, data, precision=HIGH)
 
 
+def major_exact(table, data):
+    head = table.astype(jnp.bfloat16)
+    tail = (table - head.astype(jnp.float32)).astype(jnp.bfloat16)
+    spec = "qk,k...->q..."
+    return (jnp.einsum(spec, head, data, preferred_element_type=jnp.float32)
+            + jnp.einsum(spec, tail, data, preferred_element_type=jnp.float32))
+
+
 def minor(data, table):
     return jnp.einsum("...b,bm->...m", data, table, precision=HIGH)
 
@@ -84,13 +92,13 @@
     f32, bf16 = jnp.float32, jnp.bfloat16
 
     send = send_blocks(key_gate, value_input, long_filter, seqs)
-    got = lax.all_to_all(send, "seq", 0, 0, tiled=True).astype(f32)
+    got = lax.all_to_all(send, "seq", 0, 0, tiled=True)
     packed_real, packed_imag = got[:, :chans], got[:, chans:]
 
     row_ids = row_list(seqs)
     cos_a, sin_a = turn_table(row_ids, np.arange(seqs), rows)
-    freq_real = major(cos_a, packed_real) + major(sin_a, packed_imag)
-    freq_imag = major(cos_a, packed_imag) - major(sin_a, packed_real)
+    freq_real = major_exact(cos_a, packed_real) + major_exact(sin_a, packed_imag)
+    freq_imag = major_exact(cos_a, packed_imag) - major_exact(sin_a, packed_real)
     cos_dev, sin_dev = turn_table(np.arange(seqs) * width, row_ids, full)
     cos_dev = lax.dynamic_index_in_dim(cos_dev, seq_index, 0, keepdims=False)[:, None, None]
     sin_dev = lax.dynamic_index_in_dim(sin_dev, seq_index, 0, keepdims=False)[:, None, None]
@@ -102,14 +110,14 @@
     spread_imag = freq_imag * cos_t - freq_real * sin_t
     spread = jnp.stack([spread_real, spread_imag], axis=1).astype(bf16)
     spread = spread.reshape(seqs, 2, 2, chans, width).transpose(0, 2, 1, 3, 4)
-    recv = lax.all_to_all(spread, "seq", 0, 0, tiled=True).astype(f32)
+    recv = lax.all_to_all(spread, "seq", 0, 0, tiled=True)
 
     cos_o, sin_o = turn_table(np.arange(seqs), np.arange(seqs), seqs)
     cos_w, sin_w = turn_table(np.arange(seqs), np.arange(width), length)
     cos_w, sin_w = cos_w[:, None, None, :], sin_w[:, None, None, :]
     cos_i, sin_i = turn_table(np.arange(width), np.arange(width), width)
     co_np, so_np = np_turns(np.arange(seqs), np.arange(seqs), seqs)
-    first = major(block_table(co_np, so_np, -1.0, True), recv.reshape((2 * seqs,) + recv.shape[2:]))
+    first = major_exact(block_table(co_np, so_np, -1.0, True), recv.reshape((2 * seqs,) + recv.shape[2:]))
     first_real, first_imag = first[:seqs], first[seqs:]
     twist_real = first_real * cos_w + first_imag * sin_w
     twist_imag = first_imag * cos_w - first_real * sin_w
@@ -180,11 +188,11 @@
     reverted_real = back_real * cos_b - back_imag * sin_b
     reverted_imag = back_imag * cos_b + back_real * sin_b
     reverted = jnp.stack([reverted_real, reverted_imag], axis=2).astype(bf16)
-    moved = lax.all_to_all(reverted, "seq", 0, 0, tiled=True).astype(f32)
+    moved = lax.all_to_all(reverted, "seq", 0, 0, tiled=True)
     moved = moved.reshape(2 * rows, pairs, width)
 
     cl_np, sl_np = np_turns(np.arange(seqs), row_ids, rows)
-    merged = major(block_table(cl_np, sl_np, 1.0, True, rows_reim_inner=True), moved)
+    merged = major_exact(block_table(cl_np, sl_np, 1.0, True, rows_reim_inner=True), moved)
     merged = merged.reshape(seqs, chans, width) * (1.0 / full)
     arrived = lax.all_to_all(merged.astype(bf16), "seq", 0, 0, tiled=True)
     conv = arrived.astype(f32).transpose(1, 0, 2).reshape(chans, length)

time: 153 us -> 155 us (1.013)
  matrix products: 21 us -> 22.7 us
    dot_general x0 -> x12, matrix products: none -> 7.51 us  [the longest x6 4.39 us: major_exact(): jnp.einsum(spec, tail, data, preferred_element_type=jnp.float32)]
    dot_general x7 -> x1, matrix products: 8.02 us -> 2.17 us  [major(): return jnp.einsum('qk,k...->q...', table, data, precision=HIGH)]
where the time goes in v2:
time: 155 us; the launch traced here: 154 us
  waiting for transfers between devices  48 us (31%)
  blocking collectives  37.8 us (24%)
  matrix products  22.7 us (15%)
  starting transfers between devices  20.4 us (13%)
  local copies, waits for them, and re-layouts  12.7 us (8%)
  other arithmetic  8.74 us (6%)
  Pallas kernels  2.7 us (2%)
    all_to_all x1, blocking collectives, body(): moved = lax.all_to_all(reverted, 'seq', 0, 0, tiled=True)  23.7 us
    all_to_all x1, waiting for transfers between devices, body(): recv = lax.all_to_all(spread, 'seq', 0, 0, tiled=True)  21.7 us
    all_to_all x1, waiting for transfers between devices, body(): got = lax.all_to_all(send, 'seq', 0, 0, tiled=True)  15.9 us
    all_to_all x1, blocking collectives, body(): arrived = lax.all_to_all(merged.astype(bf16), 'seq', 0, 0, tiled=True)  14.1 us
    all_to_all x1, starting transfers between devices, body(): got = lax.all_to_all(send, 'seq', 0, 0, tiled=True)  9.84 us
    ppermute x1, waiting for transfers between devices, body(): gated_far = lax.ppermute(gated_out, 'tp', cross)  9.31 us
    dot_general x2, matrix products, minor(): return jnp.einsum('...b,bm->...m', data, table, precision=HIGH)  4.94 us
    dot_general x6, matrix products, major_exact(): jnp.einsum(spec, tail, data, preferred_element_type=jnp.float32)  4.39 us
  transfers between devices with their start and end apart: 4, of which 4 were waited for; matrix products, arithmetic and copies ran while one was open for 5% of the time, Pallas kernels for 0%

profile of v2, /device:TPU:1, one launch (start us, length us, event | category | flops | bytes accessed | tf_op | source)
XLA Modules:
  0.0 153.5 jit_solution(2503373210817436380)
XLA Ops:
  0.0 2.7 %shard_map.208 = bf16[32,128,128]{2,1,0:T(8,128)(2,1)} custom-call(bf16[64,4096]{1,0:T(8,128)(2,1)} %key_ref.1, bf16[64,4096]{1,0:T(8,128)(2,1)} %value_ref.1, f32[64,4096]{1,0:T(8,128)} %taps_ref.1), custom_call_target="tpu_custom_call" | custom-call | tf_op jit(solution)/shard_map/pallas_call | solution.py:77
  2.7 9.8 %all-to-all-start = ((bf16[32,128,128]{2,1,0:T(8,128)(2,1)}), bf16[32,128,128]{2,1,0:T(8,128)(2,1)S(1)}, u32[]{:S(2)}, u32[]{:S(2)}) async-start(bf16[32,128,128]{2,1,0:T(8,128)(2,1)} %shard_map.208), calls=%async_computation | async-start | bytes 2097152 | tf_op jit(solution)/shard_map/all_to_all | solution.py:95
  12.6 0.7 fusion.74
  13.3 0.1 multiply_subtract_fusion.2
  13.4 15.9 %all-to-all-done = bf16[32,128,128]{2,1,0:T(8,128)(2,1)S(1)} async-done(((bf16[32,128,128]{2,1,0:T(8,128)(2,1)}), bf16[32,128,128]{2,1,0:T(8,128)(2,1)S(1)}, u32[]{:S(2)}, u32[]{:S(2)}) %all-to-all-start) | async-done | bytes 1048608 | tf_op jit(solution)/shard_map/all_to_all | solution.py:95
  29.3 0.5 fusion.43
  29.8 0.5 fusion.45
  30.3 0.5 fusion.33
  30.8 0.5 fusion.35
  31.3 0.5 fusion.38
  31.8 0.5 fusion.41
  32.3 0.9 add_add_fusion
  33.2 1.4 add_convert_fusion
  34.6 3.4 %copy_bitcast_fusion = bf16[32,2,2,64,128]{4,2,3,1,0:T(2,128)(2,1)} fusion(bf16[32,2,1,64,128]{4,1,0,3,2:T(2,128)(2,1)S(1)} %bitcast.116, bf16[32,2,1,64,128]{4,1,0,3,2:T(2,128)(2,1)S(1)} %bitcast.115), kind=kLoop, calls=%fused_computation.23 | loop fusion | flops 1048576 | bytes 4194304 | tf_op jit(solution)/shard_map/transpose | solution.py:112
  38.0 4.2 %all-to-all-start.1 = ((bf16[32,2,2,64,128]{4,2,3,1,0:T(2,128)(2,1)}), bf16[32,2,2,64,128]{4,2,3,1,0:T(2,128)(2,1)S(1)}, u32[]{:S(2)}, u32[]{:S(2)}) async-start(bf16[32,2,2,64,128]{4,2,3,1,0:T(2,128)(2,1)} %copy_bitcast_fusion), calls=%async_computation.1 | async-start | bytes 4194304 | tf_op jit(solution)/shard_map/all_to_all | solution.py:113
  42.2 0.1 fusion.52
  42.4 1.3 gather_fusion
  43.8 1.3 gather_fusion.2
  45.1 1.3 gather_fusion.1
  46.4 1.3 gather_fusion.3
  47.8 0.1 select_bitcast_fusion.1
  47.9 0.1 multiply_subtract_fusion.1
  48.0 21.7 %all-to-all-done.1 = bf16[32,2,2,64,128]{4,2,3,1,0:T(2,128)(2,1)S(1)} async-done(((bf16[32,2,2,64,128]{4,2,3,1,0:T(2,128)(2,1)}), bf16[32,2,2,64,128]{4,2,3,1,0:T(2,128)(2,1)S(1)}, u32[]{:S(2)}, u32[]{:S(2)}) %all-to-all-start.1) | async-done | bytes 2097184 | tf_op jit(solution)/shard_map/all_to_all | solution.py:113
  69.7 2.2 %copy.97 = bf16[32,2,2,64,128]{4,1,0,3,2:T(2,128)(2,1)S(1)} copy(bf16[32,2,2,64,128]{4,2,3,1,0:T(2,128)(2,1)S(1)} %all-to-all-done.1) | data formatting | bytes 4194304 | tf_op jit(solution)/shard_map/all_to_all | solution.py:113
  71.9 0.7 fusion.79
  72.6 0.7 convolution_add_fusion.2
  73.3 0.6 multiply_add_fusion
  73.9 0.4 pad_maximum_fusion
  74.4 0.5 copy-done.3
  74.9 3.9 %fusion.3 = f32[32,2,64,256]{3,2,1,0:T(8,128)S(1)} fusion(f32[256,256,1,1]{1,0,3,2:T(8,128)S(1)} %copy-done.3, f32[32,2,64,256]{3,0,2,1:T(8,128)S(1)} %pad_maximum_fusion), kind=kOutput, calls=%fused_computation.10 | convolution fusion | flops 1610612736 | bytes 8650752 | tf_op jit(solution)/shard_map/...b,bm->...m/dot_general | solution.py:58
  78.8 0.7 fusion.17
  79.5 0.7 fusion.19
  80.3 2.2 %fusion.9 = f32[32,2,64,128]{3,0,2,1:T(8,128)S(1)} fusion(f32[64,64,128]{2,1,0:T(8,128)S(1)} %bitcast.114, pred[32,2,64,1]{2,1,0,3:T(4,128)(4,1)S(1)} %bitcast.118), kind=kOutput, calls=%fused_computation.19 | convolution fusion | flops 201326592 | bytes 4198400 | tf_op jit(solution)/shard_map/uv,vcb->ucb/dot_general | solution.py:147
  82.4 1.2 copy.106
  83.7 2.0 %fusion.11 = f32[32,2,64,128]{3,0,2,1:T(8,128)S(1)} fusion(f32[64,64,128]{2,1,0:T(8,128)S(1)} %bitcast.112, pred[32,2,64,1]{2,1,0,3:T(4,128)(4,1)S(1)} %bitcast.119), kind=kOutput, calls=%fused_computation.21 | convolution fusion | flops 201326592 | bytes 4198400 | tf_op jit(solution)/shard_map/uv,vcb->ucb/dot_general | solution.py:147
  85.6 1.2 copy.102
  86.9 0.1 fusion.24
  87.0 0.1 fusion.26
  87.2 1.6 %add_multiply_fusion.1 = (f32[32,2,64,128]{3,2,1,0:T(8,128)S(1)}, f32[32,2,64,128]{3,2,1,0:T(8,128)S(1)}, f32[32,2,64,128]{3,2,1,0:T(8,128)S(1)}, f32[32,2,64,128]{3,2,1,0:T(8,128)S(1)}) fusion(f32[32,2,64,128]{3,2,1,0:T(8,128)S(1)} %fusion.26, f32[32,2,64,256]{3,2,1,0:T(8,128)S(1)} %fusion.3, f32[32,2,64,128]{3,2,1,0:T(8,128)S(1)} %fusion.24), kind=kLoop, calls=%fused_computation.31 | loop fusion | flops 4194304 | bytes 16777216 | tf_op jit(solution)/shard_map/mul | solution.py:156
  88.8 1.1 add_subtract_fusion.1
  89.9 1.0 fusion.5
  90.9 0.3 subtract_bitcast_fusion
  91.2 0.3 pad_maximum_fusion.2
  91.6 0.4 copy-done.6
  92.0 2.2 %fusion.13 = f32[64,2,32,128]{3,0,2,1:T(8,128)S(1)} fusion(f32[64,64,1,1]{1,0,3,2:T(8,128)S(1)} %copy-done.6, f32[64,2,32,128]{3,2,1,0:T(8,128)S(1)} %bitcast.113), kind=kOutput, calls=%fused_computation.24 | convolution fusion | flops 201326592 | bytes 4210688 | tf_op jit(solution)/shard_map/qk,k...->q.../dot_general | solution.py:46
  94.2 0.3 fusion.31
  94.5 0.1 pad_maximum_fusion.3
  94.6 0.4 copy.108
  95.0 23.7 %all_to_all.20 = bf16[32,2,2,32,128]{4,3,1,2,0:T(8,128)(2,1)S(1)} all-to-all(bf16[32,2,2,32,128]{4,3,1,2,0:T(8,128)(2,1)S(1)} %copy.108), channel_id=1, replica_groups=mesh['seq'=32,'tp'=4] {'seq'}, dimensions={0} | all-to-all | bytes 2097152 | tf_op jit(solution)/shard_map/all_to_all | solution.py:191
  118.7 0.1 copy.109
  118.8 0.5 fusion.29
  119.3 0.1 copy-done.13
  119.4 0.5 fusion.22
  119.9 0.3 copy.112
  120.3 14.1 %all_to_all.21 = bf16[32,64,128]{2,1,0:T(8,128)(2,1)S(1)} all-to-all(bf16[32,64,128]{2,1,0:T(8,128)(2,1)S(1)} %bitcast.117), channel_id=1, replica_groups=mesh['seq'=32,'tp'=4] {'seq'}, dimensions={0} | all-to-all | bytes 1048576 | tf_op jit(solution)/shard_map/all_to_all | solution.py:197
  134.4 0.1 fusion.27
  134.5 2.7 %collective-permute-start = (bf16[64,4096]{1,0:T(8,128)(2,1)S(1)}, bf16[64,4096]{1,0:T(8,128)(2,1)S(1)}, u32[]{:S(2)}, u32[]{:S(2)}) collective-permute-start(bf16[64,4096]{1,0:T(8,128)(2,1)S(1)} %fusion.27), channel_id=1, source_target_pairs={{0,2},{1,3},{2,0},{3,1},{4,6},{5,7},{6,4},{7,5},{8,10},{9,11},{10,... | collective-permute-start | bytes 1572872 | tf_op jit(solution)/shard_map/ppermute | solution.py:206
  137.2 0.4 fusion.67
  137.5 9.3 %collective-permute-done = bf16[64,4096]{1,0:T(8,128)(2,1)S(1)} collective-permute-done((bf16[64,4096]{1,0:T(8,128)(2,1)S(1)}, bf16[64,4096]{1,0:T(8,128)(2,1)S(1)}, u32[]{:S(2)}, u32[]{:S(2)}) %collective-permute-start) | collective-permute-done | bytes 524320 | tf_op jit(solution)/shard_map/ppermute | solution.py:206
  146.8 0.4 fusion.2
  147.2 3.6 %collective-permute-start.1 = (bf16[64,4096]{1,0:T(8,128)(2,1)S(1)}, bf16[64,4096]{1,0:T(8,128)(2,1)S(1)}, u32[]{:S(2)}, u32[]{:S(2)}) collective-permute-start(bf16[64,4096]{1,0:T(8,128)(2,1)S(1)} %fusion.2), channel_id=1, source_target_pairs={{0,1},{1,0},{2,3},{3,2},{4,5},{5,4},{6,7},{7,6},{8,9},{9,8},{10,11... | collective-permute-start | bytes 1572872 | tf_op jit(solution)/shard_map/ppermute | solution.py:219
  150.8 0.4 fusion.70
  151.2 1.2 collective-permute-done.1
  152.4 1.1 fusion.1
  (44 shorter events, 0.4 us)
Async XLA Ops:
  0.0 137.2 %copy-start = (bf16[256,256]{1,0:T(8,128)(2,1)S(1)}, bf16[256,256]{1,0:T(8,128)(2,1)}, u32[]{:S(2)}) copy-start(bf16[256,256]{1,0:T(8,128)(2,1)} %param.34) | copy-start | bytes 393220
  0.0 13.3 %copy-start.11 = (f32[64,128]{1,0:T(8,128)S(1)}, f32[64,128]{1,0:T(8,128)}, u32[]{:S(2)}) copy-start(f32[64,128]{1,0:T(8,128)} %constant.193.clone) | copy-start | bytes 98308
  0.0 13.3 %copy-start.12 = (f32[64,128]{1,0:T(8,128)S(1)}, f32[64,128]{1,0:T(8,128)}, u32[]{:S(2)}) copy-start(f32[64,128]{1,0:T(8,128)} %constant.194.clone) | copy-start | bytes 98308
  2.7 26.6 %copy-start.10 = (bf16[64,32,1]{0,1,2:T(8,128)(2,1)S(1)}, bf16[64,32,1]{0,1,2:T(8,128)(2,1)}, u32[]{:S(2)}) copy-start(bf16[64,32,1]{0,1,2:T(8,128)(2,1)} %constant.233) | copy-start | bytes 12292
  2.7 26.5 %all-to-all-start = ((bf16[32,128,128]{2,1,0:T(8,128)(2,1)}), bf16[32,128,128]{2,1,0:T(8,128)(2,1)S(1)}, u32[]{:S(2)}, u32[]{:S(2)}) async-start(bf16[32,128,128]{2,1,0:T(8,128)(2,1)} %shard_map.208), calls=%async_computation | async-start | bytes 2097152 | tf_op jit(solution)/shard_map/all_to_all | solution.py:95
  13.4 16.4 %copy-start.9 = (bf16[64,32,1]{0,1,2:T(8,128)(2,1)S(1)}, bf16[64,32,1]{0,1,2:T(8,128)(2,1)}, u32[]{:S(2)}) copy-start(bf16[64,32,1]{0,1,2:T(8,128)(2,1)} %constant.232) | copy-start | bytes 12292
  30.3 1.0 copy-start.8
  31.3 1.0 copy-start.7
  38.0 31.7 %all-to-all-start.1 = ((bf16[32,2,2,64,128]{4,2,3,1,0:T(2,128)(2,1)}), bf16[32,2,2,64,128]{4,2,3,1,0:T(2,128)(2,1)S(1)}, u32[]{:S(2)}, u32[]{:S(2)}) async-start(bf16[32,2,2,64,128]{4,2,3,1,0:T(2,128)(2,1)} %copy_bitcast_fusion), calls=%async_computation.1 | async-start | bytes 4194304 | tf_op jit(solution)/shard_map/all_to_all | solution.py:113
  48.0 23.9 %copy-start.16 = (bf16[64,64,1,1]{1,0,3,2:T(8,128)(2,1)S(1)}, bf16[64,64,1,1]{1,0,3,2:T(8,128)(2,1)}, u32[]{:S(2)}) copy-start(bf16[64,64,1,1]{1,0,3,2:T(8,128)(2,1)} %constant.231) | copy-start | bytes 24580
  71.9 0.7 copy-start.15
  72.6 0.7 copy-start.4
  72.6 0.7 copy-start.5
  73.9 1.0 copy-start.3
  88.8 1.1 copy-start.2
  91.2 0.8 copy-start.6
  95.0 23.9 %copy-start.14 = (bf16[64,128,1]{1,0,2:T(8,128)(2,1)S(1)}, bf16[64,128,1]{1,0,2:T(8,128)(2,1)}, u32[]{:S(2)}) copy-start(bf16[64,128,1]{1,0,2:T(8,128)(2,1)} %constant.229) | copy-start | bytes 49156
  118.7 0.7 copy-start.13
  119.4 14.9 %copy-start.1 = (bf16[64,4096]{1,0:T(8,128)(2,1)S(1)}, bf16[64,4096]{1,0:T(8,128)(2,1)}, u32[]{:S(2)}) copy-start(bf16[64,4096]{1,0:T(8,128)(2,1)} %param.30) | copy-start | bytes 1572868
  134.5 12.3 %collective-permute-start = (bf16[64,4096]{1,0:T(8,128)(2,1)S(1)}, bf16[64,4096]{1,0:T(8,128)(2,1)S(1)}, u32[]{:S(2)}, u32[]{:S(2)}) collective-permute-start(bf16[64,4096]{1,0:T(8,128)(2,1)S(1)} %fusion.27), channel_id=1, source_target_pairs={{0,2},{1,3},{2,0},{3,1},{4,6},{5,7},{6,4},{7,5},{8,10},{9,11},{10,... | collective-permute-start | bytes 1572872 | tf_op jit(solution)/shard_map/ppermute | solution.py:206
  147.2 5.2 %collective-permute-start.1 = (bf16[64,4096]{1,0:T(8,128)(2,1)S(1)}, bf16[64,4096]{1,0:T(8,128)(2,1)S(1)}, u32[]{:S(2)}, u32[]{:S(2)}) collective-permute-start(bf16[64,4096]{1,0:T(8,128)(2,1)S(1)} %fusion.2), channel_id=1, source_target_pairs={{0,1},{1,0},{2,3},{3,2},{4,5},{5,4},{6,7},{7,6},{8,9},{9,8},{10,11... | collective-permute-start | bytes 1572872 | tf_op jit(solution)/shard_map/ppermute | solution.py:219

commit v3 on v0

--- a/solution.py
+++ b/solution.py
@@ -137,13 +137,20 @@
     def negated(spec):
         flipped = jnp.einsum("...b,bm->...m", spec, lane_flip, precision=HIGH)
         moved = jnp.einsum(
-            "uv,vcb->ucb", regroup, flipped.reshape(rows, chans, width), precision=HIGH
+            "uv,vcb->ucb", regroup, flipped.reshape(rows, chans, 2 * width), precision=HIGH
         ).reshape(spec.shape)
         corner = jnp.einsum("cb,bm->cm", spec[0, 0], lane_neg, precision=HIGH)
         return moved.at[0, 0].set(jnp.where(first_dev, corner, moved[0, 0]))
 
-    neg_real = negated(spec_real)
-    neg_imag = negated(spec_imag)
+    zeros = jnp.zeros_like(lane_flip)
+    lane_flip = jnp.concatenate(
+        [jnp.concatenate([lane_flip, zeros], axis=1), jnp.concatenate([zeros, lane_flip], axis=1)], axis=0
+    )
+    lane_neg = jnp.concatenate(
+        [jnp.concatenate([lane_neg, zeros], axis=1), jnp.concatenate([zeros, lane_neg], axis=1)], axis=0
+    )
+    neg = negated(spec)
+    neg_real, neg_imag = neg[..., :width], neg[..., width:]
 
     a_real = 0.5 * (spec_real + neg_real)
     a_imag = 0.5 * (spec_imag - neg_imag)

time: 153 us -> 153 us (level)
    dot_general x2 -> x1, matrix products: 4.16 us -> 4.07 us  [negated(): jnp.einsum('uv,vcb->ucb', regroup, flipped.reshape(rows, chans, 2 * width...]
where the time goes in v3:
time: 153 us; the launch traced here: 152 us
  waiting for transfers between devices  48.1 us (31%)
  blocking collectives  37.8 us (25%)
  matrix products  21.3 us (14%)
  starting transfers between devices  20.4 us (13%)
  local copies, waits for them, and re-layouts  12.5 us (8%)
  other arithmetic  8.34 us (5%)
  Pallas kernels  2.7 us (2%)
    all_to_all x1, blocking collectives, body(): moved = lax.all_to_all(reverted, 'seq', 0, 0, tiled=True).astype(f32)  23.7 us
    all_to_all x1, waiting for transfers between devices, body(): recv = lax.all_to_all(spread, 'seq', 0, 0, tiled=True).astype(f32)  21.7 us
    all_to_all x1, waiting for transfers between devices, body(): got = lax.all_to_all(send, 'seq', 0, 0, tiled=True).astype(f32)  15.9 us
    all_to_all x1, blocking collectives, body(): arrived = lax.all_to_all(merged.astype(bf16), 'seq', 0, 0, tiled=True)  14.1 us
    all_to_all x1, starting transfers between devices, body(): got = lax.all_to_all(send, 'seq', 0, 0, tiled=True).astype(f32)  9.84 us
    ppermute x1, waiting for transfers between devices, body(): gated_far = lax.ppermute(gated_out, 'tp', cross)  9.35 us
    dot_general x7, matrix products, major(): return jnp.einsum('qk,k...->q...', table, data, precision=HIGH)  8.01 us
    dot_general x2, matrix products, minor(): return jnp.einsum('...b,bm->...m', data, table, precision=HIGH)  4.94 us
  transfers between devices with their start and end apart: 4, of which 4 were waited for; matrix products, arithmetic and copies ran while one was open for 5% of the time, Pallas kernels for 0%

profile of v3, /device:TPU:1, one launch (start us, length us, event | category | flops | bytes accessed | tf_op | source)
XLA Modules:
  0.0 151.6 jit_solution(6718856360211791408)
XLA Ops:
  0.0 2.7 %shard_map.208 = bf16[32,128,128]{2,1,0:T(8,128)(2,1)} custom-call(bf16[64,4096]{1,0:T(8,128)(2,1)} %key_ref.1, bf16[64,4096]{1,0:T(8,128)(2,1)} %value_ref.1, f32[64,4096]{1,0:T(8,128)} %taps_ref.1), custom_call_target="tpu_custom_call" | custom-call | tf_op jit(solution)/shard_map/pallas_call | solution.py:69
  2.7 9.8 %all-to-all-start = ((bf16[32,128,128]{2,1,0:T(8,128)(2,1)}), bf16[32,128,128]{2,1,0:T(8,128)(2,1)S(1)}, u32[]{:S(2)}, u32[]{:S(2)}) async-start(bf16[32,128,128]{2,1,0:T(8,128)(2,1)} %shard_map.208), calls=%async_computation | async-start | bytes 2097152 | tf_op jit(solution)/shard_map/all_to_all | solution.py:87
  12.6 0.7 fusion.62
  13.3 0.1 multiply_subtract_fusion.2
  13.4 15.9 %all-to-all-done = bf16[32,128,128]{2,1,0:T(8,128)(2,1)S(1)} async-done(((bf16[32,128,128]{2,1,0:T(8,128)(2,1)}), bf16[32,128,128]{2,1,0:T(8,128)(2,1)S(1)}, u32[]{:S(2)}, u32[]{:S(2)}) %all-to-all-start) | async-done | bytes 1048608 | tf_op jit(solution)/shard_map/all_to_all | solution.py:87
  29.3 0.1 fusion.72
  29.3 0.0 copy-start.6
  29.4 0.8 fusion.30
  30.1 0.8 fusion.26
  30.9 0.9 convolution_add_fusion.2
  31.9 1.4 fusion.13
  33.3 3.4 %copy_bitcast_fusion = bf16[32,2,2,64,128]{4,2,3,1,0:T(2,128)(2,1)} fusion(bf16[32,2,1,64,128]{4,1,0,3,2:T(2,128)(2,1)S(1)} %bitcast.106, bf16[32,2,1,64,128]{4,1,0,3,2:T(2,128)(2,1)S(1)} %bitcast.105), kind=kLoop, calls=%fused_computation.21 | loop fusion | flops 1048576 | bytes 4194304 | tf_op jit(solution)/shard_map/transpose | solution.py:104
  36.7 4.2 %all-to-all-start.1 = ((bf16[32,2,2,64,128]{4,2,3,1,0:T(2,128)(2,1)}), bf16[32,2,2,64,128]{4,2,3,1,0:T(2,128)(2,1)S(1)}, u32[]{:S(2)}, u32[]{:S(2)}) async-start(bf16[32,2,2,64,128]{4,2,3,1,0:T(2,128)(2,1)} %copy_bitcast_fusion), calls=%async_computation.1 | async-start | bytes 4194304 | tf_op jit(solution)/shard_map/all_to_all | solution.py:105
  40.9 0.1 fusion.49
  41.1 1.3 gather_fusion
  42.5 1.3 gather_fusion.2
  43.8 1.3 gather_fusion.1
  45.1 1.3 gather_fusion.3
  46.4 0.1 select_bitcast_fusion.1
  46.5 0.1 broadcast_select_fusion.1
  46.6 0.1 multiply_subtract_fusion.1
  46.7 0.0 copy-start.9
  46.7 21.7 %all-to-all-done.1 = bf16[32,2,2,64,128]{4,2,3,1,0:T(2,128)(2,1)S(1)} async-done(((bf16[32,2,2,64,128]{4,2,3,1,0:T(2,128)(2,1)}), bf16[32,2,2,64,128]{4,2,3,1,0:T(2,128)(2,1)S(1)}, u32[]{:S(2)}, u32[]{:S(2)}) %all-to-all-start.1) | async-done | bytes 2097184 | tf_op jit(solution)/shard_map/all_to_all | solution.py:105
  68.4 2.2 %copy.68 = bf16[32,2,2,64,128]{4,1,0,3,2:T(2,128)(2,1)S(1)} copy(bf16[32,2,2,64,128]{4,2,3,1,0:T(2,128)(2,1)S(1)} %all-to-all-done.1) | data formatting | bytes 4194304 | tf_op jit(solution)/shard_map/all_to_all | solution.py:105
  70.6 0.0 copy-start.4
  70.6 0.0 copy-start.5
  70.6 1.2 fusion.73
  71.9 0.6 multiply_add_fusion
  72.5 0.0 copy-start.3
  72.5 0.4 pad_maximum_fusion
  72.9 0.5 copy-done.3
  73.4 3.9 %fusion.6 = f32[32,2,64,256]{3,2,1,0:T(8,128)S(1)} fusion(f32[256,256,1,1]{1,0,3,2:T(8,128)S(1)} %copy-done.3, f32[32,2,64,256]{3,0,2,1:T(8,128)S(1)} %pad_maximum_fusion), kind=kOutput, calls=%fused_computation.13 | convolution fusion | flops 1610612736 | bytes 8650752 | tf_op jit(solution)/shard_map/...b,bm->...m/dot_general | solution.py:50
  77.4 1.9 %fusion.36 = f32[32,2,64,256]{3,2,1,0:T(8,128)S(1)} fusion(f32[32,2,64,256]{3,2,1,0:T(8,128)S(1)} %fusion.6, f32[128,128]{1,0:T(8,128)S(1)} %fusion.45), kind=kOutput, calls=%fused_computation.71 | convolution fusion | flops 1610940416 | bytes 8454144 | tf_op jit(solution)/shard_map/...b,bm->...m/dot_general | solution.py:138
  79.3 4.1 %fusion.3 = f32[32,2,64,256]{3,0,2,1:T(8,128)S(1)} fusion(f32[64,64,256]{2,1,0:T(8,128)S(1)} %bitcast.101, pred[32,2,64,1]{2,1,0,3:T(4,128)(4,1)S(1)} %bitcast.108), kind=kOutput, calls=%fused_computation.10 | convolution fusion | flops 402653184 | bytes 8392704 | tf_op jit(solution)/shard_map/uv,vcb->ucb/dot_general | solution.py:139
  83.4 2.4 %copy.73 = f32[32,2,64,256]{3,2,1,0:T(8,128)S(1)} copy(f32[32,2,64,256]{3,0,2,1:T(8,128)S(1)} %fusion.3) | data formatting | bytes 8388608 | tf_op jit(solution)/shard_map/uv,vcb->ucb/dot_general | solution.py:139
  85.8 0.2 fusion.21
  86.1 1.2 add_multiply_fusion.1
  87.3 0.0 copy-start.2
  87.3 1.1 add_subtract_fusion
  88.3 1.0 fusion.8
  89.4 0.3 subtract_bitcast_fusion
  89.7 0.0 copy-start.8
  89.7 0.3 pad_maximum_fusion.2
  90.0 0.4 copy-done.8
  90.5 2.2 %fusion.16 = f32[64,2,32,128]{3,0,2,1:T(8,128)S(1)} fusion(f32[64,64,1,1]{1,0,3,2:T(8,128)S(1)} %copy-done.8, f32[64,2,32,128]{3,2,1,0:T(8,128)S(1)} %bitcast.103), kind=kOutput, calls=%fused_computation.30 | convolution fusion | flops 201326592 | bytes 4210688 | tf_op jit(solution)/shard_map/qk,k...->q.../dot_general | solution.py:46
  92.6 0.3 fusion.24
  92.9 0.1 pad_maximum_fusion.3
  93.0 0.4 copy.75
  93.4 0.0 copy-start.10
  93.5 23.7 %all_to_all.20 = bf16[32,2,2,32,128]{4,3,1,2,0:T(8,128)(2,1)S(1)} all-to-all(bf16[32,2,2,32,128]{4,3,1,2,0:T(8,128)(2,1)S(1)} %copy.75), channel_id=1, replica_groups=mesh['seq'=32,'tp'=4] {'seq'}, dimensions={0} | all-to-all | bytes 2097152 | tf_op jit(solution)/shard_map/all_to_all | solution.py:190
  117.2 0.1 copy.76
  117.3 0.0 copy-start.1
  117.3 0.7 fusion.19
  118.0 0.3 copy.78
  118.4 14.1 %all_to_all.21 = bf16[32,64,128]{2,1,0:T(8,128)(2,1)S(1)} all-to-all(bf16[32,64,128]{2,1,0:T(8,128)(2,1)S(1)} %bitcast.107), channel_id=1, replica_groups=mesh['seq'=32,'tp'=4] {'seq'}, dimensions={0} | all-to-all | bytes 1048576 | tf_op jit(solution)/shard_map/all_to_all | solution.py:196
  132.5 0.1 fusion.22
  132.6 2.7 %collective-permute-start = (bf16[64,4096]{1,0:T(8,128)(2,1)S(1)}, bf16[64,4096]{1,0:T(8,128)(2,1)S(1)}, u32[]{:S(2)}, u32[]{:S(2)}) collective-permute-start(bf16[64,4096]{1,0:T(8,128)(2,1)S(1)} %fusion.22), channel_id=1, source_target_pairs={{0,2},{1,3},{2,0},{3,1},{4,6},{5,7},{6,4},{7,5},{8,10},{9,11},{10,... | collective-permute-start | bytes 1572872 | tf_op jit(solution)/shard_map/ppermute | solution.py:205
  135.2 0.3 fusion.57
  135.6 9.3 %collective-permute-done = bf16[64,4096]{1,0:T(8,128)(2,1)S(1)} collective-permute-done((bf16[64,4096]{1,0:T(8,128)(2,1)S(1)}, bf16[64,4096]{1,0:T(8,128)(2,1)S(1)}, u32[]{:S(2)}, u32[]{:S(2)}) %collective-permute-start) | collective-permute-done | bytes 524320 | tf_op jit(solution)/shard_map/ppermute | solution.py:205
  144.9 0.3 fusion.2
  145.3 3.7 %collective-permute-start.1 = (bf16[64,4096]{1,0:T(8,128)(2,1)S(1)}, bf16[64,4096]{1,0:T(8,128)(2,1)S(1)}, u32[]{:S(2)}, u32[]{:S(2)}) collective-permute-start(bf16[64,4096]{1,0:T(8,128)(2,1)S(1)} %fusion.2), channel_id=1, source_target_pairs={{0,1},{1,0},{2,3},{3,2},{4,5},{5,4},{6,7},{7,6},{8,9},{9,8},{10,11... | collective-permute-start | bytes 1572872 | tf_op jit(solution)/shard_map/ppermute | solution.py:218
  149.0 0.3 fusion.60
  149.3 1.2 collective-permute-done.1
  150.5 1.2 fusion.1
  (27 shorter events, 0.1 us)
Async XLA Ops:
  0.0 135.2 %copy-start = (bf16[256,256]{1,0:T(8,128)(2,1)S(1)}, bf16[256,256]{1,0:T(8,128)(2,1)}, u32[]{:S(2)}) copy-start(bf16[256,256]{1,0:T(8,128)(2,1)} %param.32) | copy-start | bytes 393220
  0.0 13.3 %copy-start.11 = (f32[64,128]{1,0:T(8,128)S(1)}, f32[64,128]{1,0:T(8,128)}, u32[]{:S(2)}) copy-start(f32[64,128]{1,0:T(8,128)} %constant.174.clone) | copy-start | bytes 98308
  0.0 13.3 %copy-start.12 = (f32[64,128]{1,0:T(8,128)S(1)}, f32[64,128]{1,0:T(8,128)}, u32[]{:S(2)}) copy-start(f32[64,128]{1,0:T(8,128)} %constant.175.clone) | copy-start | bytes 98308
  2.7 26.6 %copy-start.7 = (f32[64,32,1]{0,1,2:T(8,128)S(1)}, f32[64,32,1]{0,1,2:T(8,128)}, u32[]{:S(2)}) copy-start(f32[64,32,1]{0,1,2:T(8,128)} %constant.204) | copy-start | bytes 24580
  2.7 26.5 %all-to-all-start = ((bf16[32,128,128]{2,1,0:T(8,128)(2,1)}), bf16[32,128,128]{2,1,0:T(8,128)(2,1)S(1)}, u32[]{:S(2)}, u32[]{:S(2)}) async-start(bf16[32,128,128]{2,1,0:T(8,128)(2,1)} %shard_map.208), calls=%async_computation | async-start | bytes 2097152 | tf_op jit(solution)/shard_map/all_to_all | solution.py:87
  29.3 1.6 %copy-start.6 = (f32[64,32,1]{0,1,2:T(8,128)S(1)}, f32[64,32,1]{0,1,2:T(8,128)}, u32[]{:S(2)}) copy-start(f32[64,32,1]{0,1,2:T(8,128)} %constant.205) | copy-start | bytes 24580
  36.7 31.7 %all-to-all-start.1 = ((bf16[32,2,2,64,128]{4,2,3,1,0:T(2,128)(2,1)}), bf16[32,2,2,64,128]{4,2,3,1,0:T(2,128)(2,1)S(1)}, u32[]{:S(2)}, u32[]{:S(2)}) async-start(bf16[32,2,2,64,128]{4,2,3,1,0:T(2,128)(2,1)} %copy_bitcast_fusion), calls=%async_computation.1 | async-start | bytes 4194304 | tf_op jit(solution)/shard_map/all_to_all | solution.py:105
  46.7 23.9 %copy-start.9 = (f32[64,64,1,1]{1,0,3,2:T(8,128)S(1)}, f32[64,64,1,1]{1,0,3,2:T(8,128)}, u32[]{:S(2)}) copy-start(f32[64,64,1,1]{1,0,3,2:T(8,128)} %constant.203) | copy-start | bytes 49156
  70.6 1.3 copy-start.4
  70.6 1.3 copy-start.5
  72.5 1.0 copy-start.3
  87.3 1.1 copy-start.2
  89.7 0.8 copy-start.8
  93.4 23.9 %copy-start.10 = (f32[64,128,1]{1,0,2:T(8,128)S(1)}, f32[64,128,1]{1,0,2:T(8,128)}, u32[]{:S(2)}) copy-start(f32[64,128,1]{1,0,2:T(8,128)} %constant.208) | copy-start | bytes 98308
  117.3 15.1 %copy-start.1 = (bf16[64,4096]{1,0:T(8,128)(2,1)S(1)}, bf16[64,4096]{1,0:T(8,128)(2,1)}, u32[]{:S(2)}) copy-start(bf16[64,4096]{1,0:T(8,128)(2,1)} %param.28) | copy-start | bytes 1572868
  132.6 12.3 %collective-permute-start = (bf16[64,4096]{1,0:T(8,128)(2,1)S(1)}, bf16[64,4096]{1,0:T(8,128)(2,1)S(1)}, u32[]{:S(2)}, u32[]{:S(2)}) collective-permute-start(bf16[64,4096]{1,0:T(8,128)(2,1)S(1)} %fusion.22), channel_id=1, source_target_pairs={{0,2},{1,3},{2,0},{3,1},{4,6},{5,7},{6,4},{7,5},{8,10},{9,11},{10,... | collective-permute-start | bytes 1572872 | tf_op jit(solution)/shard_map/ppermute | solution.py:205
  145.3 5.2 %collective-permute-start.1 = (bf16[64,4096]{1,0:T(8,128)(2,1)S(1)}, bf16[64,4096]{1,0:T(8,128)(2,1)S(1)}, u32[]{:S(2)}, u32[]{:S(2)}) collective-permute-start(bf16[64,4096]{1,0:T(8,128)(2,1)S(1)} %fusion.2), channel_id=1, source_target_pairs={{0,1},{1,0},{2,3},{3,2},{4,5},{5,4},{6,7},{7,6},{8,9},{9,8},{10,11... | collective-permute-start | bytes 1572872 | tf_op jit(solution)/shard_map/ppermute | solution.py:218

commit v4 on v3

--- a/solution.py
+++ b/solution.py
@@ -48,6 +48,14 @@
 
 def minor(data, table):
     return jnp.einsum("...b,bm->...m", data, table, precision=HIGH)
+
+
+def permuted(spec, data, table):
+    head = data.astype(jnp.bfloat16)
+    tail = (data - head.astype(jnp.float32)).astype(jnp.bfloat16)
+    perm = table.astype(jnp.bfloat16)
+    return (jnp.einsum(spec, head, perm, preferred_element_type=jnp.float32)
+            + jnp.einsum(spec, tail, perm, preferred_element_type=jnp.float32))
 
 
 def send_blocks(key_gate, value_input, long_filter, seqs, interpret=False):
@@ -135,11 +143,9 @@
     regroup = (source == jnp.where(first_dev, self_src, cross_src)).astype(f32)
 
     def negated(spec):
-        flipped = jnp.einsum("...b,bm->...m", spec, lane_flip, precision=HIGH)
-        moved = jnp.einsum(
-            "uv,vcb->ucb", regroup, flipped.reshape(rows, chans, 2 * width), precision=HIGH
-        ).reshape(spec.shape)
-        corner = jnp.einsum("cb,bm->cm", spec[0, 0], lane_neg, precision=HIGH)
+        flipped = permuted("...b,bm->...m", spec, lane_flip)
+        moved = permuted("vcb,uv->ucb", flipped.reshape(rows, chans, 2 * width), regroup).reshape(spec.shape)
+        corner = permuted("cb,bm->cm", spec[0, 0], lane_neg)
         return moved.at[0, 0].set(jnp.where(first_dev, corner, moved[0, 0]))
 
     zeros = jnp.zeros_like(lane_flip)

time: 153 us -> 154 us (level)
    dot_general x1 -> x0, local copies, waits for them, and re-layouts: 2.43 us -> none  [negated(): jnp.einsum('uv,vcb->ucb', regroup, flipped.reshape(rows, chans, 2 * width...]
    add x0 -> x1, local copies, waits for them, and re-layouts: none -> 2.43 us  [permuted(): jnp.einsum(spec, head, perm, preferred_element_type=jnp.float32)]
    dot_general x3 -> x6, matrix products: 6.21 us -> 7.66 us  [the longest x3 3.89 us: permuted(): jnp.einsum(spec, tail, perm, preferred_element_type=jnp.float32)]
where the time goes in v4:
time: 154 us; the launch traced here: 153 us
  waiting for transfers between devices  48.2 us (31%)
  blocking collectives  38 us (25%)
  matrix products  22.8 us (15%)
  starting transfers between devices  20.4 us (13%)
  local copies, waits for them, and re-layouts  12.5 us (8%)
  other arithmetic  8.24 us (5%)
  Pallas kernels  2.7 us (2%)
    all_to_all x1, blocking collectives, body(): moved = lax.all_to_all(reverted, 'seq', 0, 0, tiled=True).astype(f32)  24 us
    all_to_all x1, waiting for transfers between devices, body(): recv = lax.all_to_all(spread, 'seq', 0, 0, tiled=True).astype(f32)  21.8 us
    all_to_all x1, waiting for transfers between devices, body(): got = lax.all_to_all(send, 'seq', 0, 0, tiled=True).astype(f32)  15.9 us
    all_to_all x1, blocking collectives, body(): arrived = lax.all_to_all(merged.astype(bf16), 'seq', 0, 0, tiled=True)  14.1 us
    all_to_all x1, starting transfers between devices, body(): got = lax.all_to_all(send, 'seq', 0, 0, tiled=True).astype(f32)  9.84 us
    ppermute x1, waiting for transfers between devices, body(): gated_far = lax.ppermute(gated_out, 'tp', cross)  9.32 us
    dot_general x7, matrix products, major(): return jnp.einsum('qk,k...->q...', table, data, precision=HIGH)  8.02 us
    dot_general x2, matrix products, minor(): return jnp.einsum('...b,bm->...m', data, table, precision=HIGH)  4.94 us
  transfers between devices with their start and end apart: 4, of which 4 were waited for; matrix products, arithmetic and copies ran while one was open for 5% of the time, Pallas kernels for 0%

profile of v4, /device:TPU:1, one launch (start us, length us, event | category | flops | bytes accessed | tf_op | source)
XLA Modules:
  0.0 153.3 jit_solution(11247401612023711005)
XLA Ops:
  0.0 2.7 %shard_map.208 = bf16[32,128,128]{2,1,0:T(8,128)(2,1)} custom-call(bf16[64,4096]{1,0:T(8,128)(2,1)} %key_ref.1, bf16[64,4096]{1,0:T(8,128)(2,1)} %value_ref.1, f32[64,4096]{1,0:T(8,128)} %taps_ref.1), custom_call_target="tpu_custom_call" | custom-call | tf_op jit(solution)/shard_map/pallas_call | solution.py:77
  2.7 9.8 %all-to-all-start = ((bf16[32,128,128]{2,1,0:T(8,128)(2,1)}), bf16[32,128,128]{2,1,0:T(8,128)(2,1)S(1)}, u32[]{:S(2)}, u32[]{:S(2)}) async-start(bf16[32,128,128]{2,1,0:T(8,128)(2,1)} %shard_map.208), calls=%async_computation | async-start | bytes 2097152 | tf_op jit(solution)/shard_map/all_to_all | solution.py:95
  12.6 0.7 fusion.74
  13.3 0.1 multiply_subtract_fusion.2
  13.4 15.9 %all-to-all-done = bf16[32,128,128]{2,1,0:T(8,128)(2,1)S(1)} async-done(((bf16[32,128,128]{2,1,0:T(8,128)(2,1)}), bf16[32,128,128]{2,1,0:T(8,128)(2,1)S(1)}, u32[]{:S(2)}, u32[]{:S(2)}) %all-to-all-start) | async-done | bytes 1048608 | tf_op jit(solution)/shard_map/all_to_all | solution.py:95
  29.3 0.1 fusion.98
  29.3 0.0 copy-start.6
  29.4 0.8 fusion.34
  30.1 0.8 fusion.30
  30.9 0.9 convolution_add_fusion.3
  31.9 1.4 fusion.13
  33.3 3.4 %copy_bitcast_fusion = bf16[32,2,2,64,128]{4,2,3,1,0:T(2,128)(2,1)} fusion(bf16[32,2,1,64,128]{4,1,0,3,2:T(2,128)(2,1)S(1)} %bitcast.118, bf16[32,2,1,64,128]{4,1,0,3,2:T(2,128)(2,1)S(1)} %bitcast.117), kind=kLoop, calls=%fused_computation.25 | loop fusion | flops 1048576 | bytes 4194304 | tf_op jit(solution)/shard_map/transpose | solution.py:112
  36.7 4.2 %all-to-all-start.1 = ((bf16[32,2,2,64,128]{4,2,3,1,0:T(2,128)(2,1)}), bf16[32,2,2,64,128]{4,2,3,1,0:T(2,128)(2,1)S(1)}, u32[]{:S(2)}, u32[]{:S(2)}) async-start(bf16[32,2,2,64,128]{4,2,3,1,0:T(2,128)(2,1)} %copy_bitcast_fusion), calls=%async_computation.1 | async-start | bytes 4194304 | tf_op jit(solution)/shard_map/all_to_all | solution.py:113
  41.0 1.3 gather_fusion
  42.3 1.3 gather_fusion.2
  43.6 1.3 gather_fusion.1
  44.9 1.3 gather_fusion.3
  46.3 0.1 select_bitcast_fusion.1
  46.4 0.1 broadcast_select_fusion.1
  46.5 0.1 multiply_subtract_fusion.1
  46.6 21.8 %all-to-all-done.1 = bf16[32,2,2,64,128]{4,2,3,1,0:T(2,128)(2,1)S(1)} async-done(((bf16[32,2,2,64,128]{4,2,3,1,0:T(2,128)(2,1)}), bf16[32,2,2,64,128]{4,2,3,1,0:T(2,128)(2,1)S(1)}, u32[]{:S(2)}, u32[]{:S(2)}) %all-to-all-start.1) | async-done | bytes 2097184 | tf_op jit(solution)/shard_map/all_to_all | solution.py:113
  68.4 2.2 %copy.66 = bf16[32,2,2,64,128]{4,1,0,3,2:T(2,128)(2,1)S(1)} copy(bf16[32,2,2,64,128]{4,2,3,1,0:T(2,128)(2,1)S(1)} %all-to-all-done.1) | data formatting | bytes 4194304 | tf_op jit(solution)/shard_map/all_to_all | solution.py:113
  70.6 0.0 copy-start.4
  70.6 0.0 copy-start.5
  70.6 1.2 fusion.99
  71.9 0.6 multiply_add_fusion
  72.5 0.0 copy-start.3
  72.5 0.4 pad_maximum_fusion
  72.9 0.5 copy-done.3
  73.4 3.9 %fusion.3 = f32[32,2,64,256]{3,2,1,0:T(8,128)S(1)} fusion(f32[256,256,1,1]{1,0,3,2:T(8,128)S(1)} %copy-done.3, f32[32,2,64,256]{3,0,2,1:T(8,128)S(1)} %pad_maximum_fusion), kind=kOutput, calls=%fused_computation.10 | convolution fusion | flops 1610612736 | bytes 8650752 | tf_op jit(solution)/shard_map/...b,bm->...m/dot_general | solution.py:50
  77.4 0.7 fusion.26
  78.1 0.7 convolution_add_fusion.2
  78.8 3.0 %fusion.7 = f32[64,64,256]{2,0,1:T(8,128)S(1)} fusion(f32[64,64,256]{2,1,0:T(8,128)S(1)} %bitcast.110, s32[64]{0:T(128)S(1)} %get-tuple-element.51, s32[64]{0:T(128)S(1)} %get-tuple-element.53, s32[64]{0:T(128)S(1)} %get-tuple-element.52, s32[64]{0:T(128)S(1)} %get-tuple-element.54, pred[64]{0:T(512)(128)(4,1)S(1)} %get-tuple-element.47, ...), kind=kOutput, calls=%fused_computation.18 | convolution fusion | flops 138514432 | bytes 8389761 | tf_op jit(solution)/shard_map/vcb,uv->ucb/dot_general | solution.py:58
  81.8 2.9 %fusion.6 = f32[64,64,256]{2,0,1:T(8,128)S(1)} fusion(f32[64,64,256]{2,0,1:T(8,128)S(1)} %fusion.7, f32[64,64,256]{2,1,0:T(8,128)S(1)} %bitcast.111, s32[64]{0:T(128)S(1)} %get-tuple-element.51, s32[64]{0:T(128)S(1)} %get-tuple-element.53, s32[64]{0:T(128)S(1)} %get-tuple-element.52, s32[64]{0:T(128)S(1)} %get-tuple-element.54, ...), kind=kOutput, calls=%fused_computation.16 | convolution fusion | flops 135368704 | bytes 12584065 | tf_op jit(solution)/shard_map/vcb,uv->ucb/dot_general | solution.py:57
  84.8 2.4 %copy.70 = f32[64,64,256]{2,1,0:T(8,128)S(1)} copy(f32[64,64,256]{2,0,1:T(8,128)S(1)} %fusion.6) | data formatting | bytes 8388608 | tf_op jit(solution)/shard_map/add | solution.py:57
  87.2 0.1 fusion.46
  87.3 0.2 fusion.22
  87.5 1.2 add_multiply_fusion.1
  88.7 0.0 copy-start.2
  88.7 1.1 add_subtract_fusion
  89.8 1.0 fusion.8
  90.8 0.3 subtract_bitcast_fusion
  91.1 0.0 copy-start.8
  91.2 0.3 pad_maximum_fusion.2
  91.5 0.4 copy-done.8
  91.9 2.2 %fusion.16 = f32[64,2,32,128]{3,0,2,1:T(8,128)S(1)} fusion(f32[64,64,1,1]{1,0,3,2:T(8,128)S(1)} %copy-done.8, f32[64,2,32,128]{3,2,1,0:T(8,128)S(1)} %bitcast.115), kind=kOutput, calls=%fused_computation.34 | convolution fusion | flops 201326592 | bytes 4210688 | tf_op jit(solution)/shard_map/qk,k...->q.../dot_general | solution.py:46
  94.1 0.3 fusion.28
  94.4 0.1 pad_maximum_fusion.3
  94.5 0.4 copy.72
  94.9 0.0 copy-start.10
  94.9 24.0 %all_to_all.20 = bf16[32,2,2,32,128]{4,3,1,2,0:T(8,128)(2,1)S(1)} all-to-all(bf16[32,2,2,32,128]{4,3,1,2,0:T(8,128)(2,1)S(1)} %copy.72), channel_id=1, replica_groups=mesh['seq'=32,'tp'=4] {'seq'}, dimensions={0} | all-to-all | bytes 2097152 | tf_op jit(solution)/shard_map/all_to_all | solution.py:196
  118.9 0.1 copy.73
  119.0 0.7 fusion.19
  119.8 0.3 copy.75
  120.1 14.1 %all_to_all.21 = bf16[32,64,128]{2,1,0:T(8,128)(2,1)S(1)} all-to-all(bf16[32,64,128]{2,1,0:T(8,128)(2,1)S(1)} %bitcast.119), channel_id=1, replica_groups=mesh['seq'=32,'tp'=4] {'seq'}, dimensions={0} | all-to-all | bytes 1048576 | tf_op jit(solution)/shard_map/all_to_all | solution.py:202
  134.2 0.1 fusion.23
  134.3 2.7 %collective-permute-start = (bf16[64,4096]{1,0:T(8,128)(2,1)S(1)}, bf16[64,4096]{1,0:T(8,128)(2,1)S(1)}, u32[]{:S(2)}, u32[]{:S(2)}) collective-permute-start(bf16[64,4096]{1,0:T(8,128)(2,1)S(1)} %fusion.23), channel_id=1, source_target_pairs={{0,2},{1,3},{2,0},{3,1},{4,6},{5,7},{6,4},{7,5},{8,10},{9,11},{10,... | collective-permute-start | bytes 1572872 | tf_op jit(solution)/shard_map/ppermute | solution.py:211
  137.0 0.4 fusion.63
  137.3 9.3 %collective-permute-done = bf16[64,4096]{1,0:T(8,128)(2,1)S(1)} collective-permute-done((bf16[64,4096]{1,0:T(8,128)(2,1)S(1)}, bf16[64,4096]{1,0:T(8,128)(2,1)S(1)}, u32[]{:S(2)}, u32[]{:S(2)}) %collective-permute-start) | collective-permute-done | bytes 524320 | tf_op jit(solution)/shard_map/ppermute | solution.py:211
  146.6 0.3 fusion.2
  147.0 3.7 %collective-permute-start.1 = (bf16[64,4096]{1,0:T(8,128)(2,1)S(1)}, bf16[64,4096]{1,0:T(8,128)(2,1)S(1)}, u32[]{:S(2)}, u32[]{:S(2)}) collective-permute-start(bf16[64,4096]{1,0:T(8,128)(2,1)S(1)} %fusion.2), channel_id=1, source_target_pairs={{0,1},{1,0},{2,3},{3,2},{4,5},{5,4},{6,7},{7,6},{8,9},{9,8},{10,11... | collective-permute-start | bytes 1572872 | tf_op jit(solution)/shard_map/ppermute | solution.py:224
  150.7 0.3 fusion.66
  151.0 1.2 collective-permute-done.1
  152.2 1.1 fusion.1
  (28 shorter events, 0.1 us)
Async XLA Ops:
  0.0 137.0 %copy-start = (bf16[256,256]{1,0:T(8,128)(2,1)S(1)}, bf16[256,256]{1,0:T(8,128)(2,1)}, u32[]{:S(2)}) copy-start(bf16[256,256]{1,0:T(8,128)(2,1)} %param.32) | copy-start | bytes 393220
  0.0 13.3 %copy-start.11 = (f32[64,128]{1,0:T(8,128)S(1)}, f32[64,128]{1,0:T(8,128)}, u32[]{:S(2)}) copy-start(f32[64,128]{1,0:T(8,128)} %constant.175.clone) | copy-start | bytes 98308
  0.0 13.3 %copy-start.12 = (f32[64,128]{1,0:T(8,128)S(1)}, f32[64,128]{1,0:T(8,128)}, u32[]{:S(2)}) copy-start(f32[64,128]{1,0:T(8,128)} %constant.176.clone) | copy-start | bytes 98308
  2.7 26.6 %copy-start.7 = (f32[64,32,1]{0,1,2:T(8,128)S(1)}, f32[64,32,1]{0,1,2:T(8,128)}, u32[]{:S(2)}) copy-start(f32[64,32,1]{0,1,2:T(8,128)} %constant.205) | copy-start | bytes 24580
  2.7 26.5 %all-to-all-start = ((bf16[32,128,128]{2,1,0:T(8,128)(2,1)}), bf16[32,128,128]{2,1,0:T(8,128)(2,1)S(1)}, u32[]{:S(2)}, u32[]{:S(2)}) async-start(bf16[32,128,128]{2,1,0:T(8,128)(2,1)} %shard_map.208), calls=%async_computation | async-start | bytes 2097152 | tf_op jit(solution)/shard_map/all_to_all | solution.py:95
  29.3 1.6 %copy-start.6 = (f32[64,32,1]{0,1,2:T(8,128)S(1)}, f32[64,32,1]{0,1,2:T(8,128)}, u32[]{:S(2)}) copy-start(f32[64,32,1]{0,1,2:T(8,128)} %constant.206) | copy-start | bytes 24580
  36.7 31.7 %all-to-all-start.1 = ((bf16[32,2,2,64,128]{4,2,3,1,0:T(2,128)(2,1)}), bf16[32,2,2,64,128]{4,2,3,1,0:T(2,128)(2,1)S(1)}, u32[]{:S(2)}, u32[]{:S(2)}) async-start(bf16[32,2,2,64,128]{4,2,3,1,0:T(2,128)(2,1)} %copy_bitcast_fusion), calls=%async_computation.1 | async-start | bytes 4194304 | tf_op jit(solution)/shard_map/all_to_all | solution.py:113
  46.6 24.0 %copy-start.9 = (f32[64,64,1,1]{1,0,3,2:T(8,128)S(1)}, f32[64,64,1,1]{1,0,3,2:T(8,128)}, u32[]{:S(2)}) copy-start(f32[64,64,1,1]{1,0,3,2:T(8,128)} %constant.204) | copy-start | bytes 49156
  70.6 1.3 copy-start.4
  70.6 1.3 copy-start.5
  72.5 1.0 copy-start.3
  88.7 1.1 copy-start.2
  91.1 0.8 copy-start.8
  94.9 24.1 %copy-start.10 = (f32[64,128,1]{1,0,2:T(8,128)S(1)}, f32[64,128,1]{1,0,2:T(8,128)}, u32[]{:S(2)}) copy-start(f32[64,128,1]{1,0,2:T(8,128)} %constant.209) | copy-start | bytes 98308
  119.0 15.1 %copy-start.1 = (bf16[64,4096]{1,0:T(8,128)(2,1)S(1)}, bf16[64,4096]{1,0:T(8,128)(2,1)}, u32[]{:S(2)}) copy-start(bf16[64,4096]{1,0:T(8,128)(2,1)} %param.28) | copy-start | bytes 1572868
  134.3 12.3 %collective-permute-start = (bf16[64,4096]{1,0:T(8,128)(2,1)S(1)}, bf16[64,4096]{1,0:T(8,128)(2,1)S(1)}, u32[]{:S(2)}, u32[]{:S(2)}) collective-permute-start(bf16[64,4096]{1,0:T(8,128)(2,1)S(1)} %fusion.23), channel_id=1, source_target_pairs={{0,2},{1,3},{2,0},{3,1},{4,6},{5,7},{6,4},{7,5},{8,10},{9,11},{10,... | collective-permute-start | bytes 1572872 | tf_op jit(solution)/shard_map/ppermute | solution.py:211
  147.0 5.2 %collective-permute-start.1 = (bf16[64,4096]{1,0:T(8,128)(2,1)S(1)}, bf16[64,4096]{1,0:T(8,128)(2,1)S(1)}, u32[]{:S(2)}, u32[]{:S(2)}) collective-permute-start(bf16[64,4096]{1,0:T(8,128)(2,1)S(1)} %fusion.2), channel_id=1, source_target_pairs={{0,1},{1,0},{2,3},{3,2},{4,5},{5,4},{6,7},{7,6},{8,9},{9,8},{10,11... | collective-permute-start | bytes 1572872 | tf_op jit(solution)/shard_map/ppermute | solution.py:224

commit v5 on v3

--- a/solution.py
+++ b/solution.py
@@ -135,10 +135,10 @@
     regroup = (source == jnp.where(first_dev, self_src, cross_src)).astype(f32)
 
     def negated(spec):
-        flipped = jnp.einsum("...b,bm->...m", spec, lane_flip, precision=HIGH)
-        moved = jnp.einsum(
-            "uv,vcb->ucb", regroup, flipped.reshape(rows, chans, 2 * width), precision=HIGH
+        regrouped = jnp.einsum(
+            "uv,vcb->ucb", regroup, spec.reshape(rows, chans, 2 * width), precision=HIGH
         ).reshape(spec.shape)
+        moved = jnp.einsum("...b,bm->...m", regrouped, lane_flip, precision=HIGH)
         corner = jnp.einsum("cb,bm->cm", spec[0, 0], lane_neg, precision=HIGH)
         return moved.at[0, 0].set(jnp.where(first_dev, corner, moved[0, 0]))
 

time: 153 us -> 152 us (level)
  local copies, waits for them, and re-layouts: 12.5 us -> 10.1 us
  matrix products: 21.3 us -> 23.4 us
    dot_general x1 -> x0, local copies, waits for them, and re-layouts: 2.43 us -> none  [negated(): jnp.einsum('uv,vcb->ucb', regroup, flipped.reshape(rows, chans, 2 * width...]
    dot_general x2, matrix products: 6 us -> 8 us  [the longest x1 4.07 us: negated(): jnp.einsum('uv,vcb->ucb', regroup, spec.reshape(rows, chans, 2 * width),...]
where the time goes in v5:
time: 152 us; the launch traced here: 151 us
  waiting for transfers between devices  48.1 us (32%)
  blocking collectives  37.8 us (25%)
  matrix products  23.4 us (15%)
  starting transfers between devices  20.4 us (13%)
  local copies, waits for them, and re-layouts  10.1 us (7%)
  other arithmetic  8.34 us (5%)
  Pallas kernels  2.7 us (2%)
    all_to_all x1, blocking collectives, body(): moved = lax.all_to_all(reverted, 'seq', 0, 0, tiled=True).astype(f32)  23.7 us
    all_to_all x1, waiting for transfers between devices, body(): recv = lax.all_to_all(spread, 'seq', 0, 0, tiled=True).astype(f32)  21.7 us
    all_to_all x1, waiting for transfers between devices, body(): got = lax.all_to_all(send, 'seq', 0, 0, tiled=True).astype(f32)  15.9 us
    all_to_all x1, blocking collectives, body(): arrived = lax.all_to_all(merged.astype(bf16), 'seq', 0, 0, tiled=True)  14.1 us
    all_to_all x1, starting transfers between devices, body(): got = lax.all_to_all(send, 'seq', 0, 0, tiled=True).astype(f32)  9.84 us
    ppermute x1, waiting for transfers between devices, body(): gated_far = lax.ppermute(gated_out, 'tp', cross)  9.33 us
    dot_general x7, matrix products, major(): return jnp.einsum('qk,k...->q...', table, data, precision=HIGH)  8.02 us
    dot_general x2, matrix products, minor(): return jnp.einsum('...b,bm->...m', data, table, precision=HIGH)  4.94 us
  transfers between devices with their start and end apart: 4, of which 4 were waited for; matrix products, arithmetic and copies ran while one was open for 5% of the time, Pallas kernels for 0%

profile of v5, /device:TPU:1, one launch (start us, length us, event | category | flops | bytes accessed | tf_op | source)
XLA Modules:
  0.0 151.2 jit_solution(16781466700846419079)
XLA Ops:
  0.0 0.0 copy-start
  0.0 2.7 %shard_map.208 = bf16[32,128,128]{2,1,0:T(8,128)(2,1)} custom-call(bf16[64,4096]{1,0:T(8,128)(2,1)} %key_ref.1, bf16[64,4096]{1,0:T(8,128)(2,1)} %value_ref.1, f32[64,4096]{1,0:T(8,128)} %taps_ref.1), custom_call_target="tpu_custom_call" | custom-call | tf_op jit(solution)/shard_map/pallas_call | solution.py:69
  2.7 9.8 %all-to-all-start = ((bf16[32,128,128]{2,1,0:T(8,128)(2,1)}), bf16[32,128,128]{2,1,0:T(8,128)(2,1)S(1)}, u32[]{:S(2)}, u32[]{:S(2)}) async-start(bf16[32,128,128]{2,1,0:T(8,128)(2,1)} %shard_map.208), calls=%async_computation | async-start | bytes 2097152 | tf_op jit(solution)/shard_map/all_to_all | solution.py:87
  12.6 0.7 fusion.63
  13.3 0.1 multiply_subtract_fusion.2
  13.4 15.9 %all-to-all-done = bf16[32,128,128]{2,1,0:T(8,128)(2,1)S(1)} async-done(((bf16[32,128,128]{2,1,0:T(8,128)(2,1)}), bf16[32,128,128]{2,1,0:T(8,128)(2,1)S(1)}, u32[]{:S(2)}, u32[]{:S(2)}) %all-to-all-start) | async-done | bytes 1048608 | tf_op jit(solution)/shard_map/all_to_all | solution.py:87
  29.3 0.1 fusion.73
  29.3 0.0 copy-start.6
  29.4 0.8 fusion.32
  30.1 0.8 fusion.28
  30.9 0.9 convolution_add_fusion.2
  31.9 1.4 fusion.15
  33.3 3.4 %copy_bitcast_fusion = bf16[32,2,2,64,128]{4,2,3,1,0:T(2,128)(2,1)} fusion(bf16[32,2,1,64,128]{4,1,0,3,2:T(2,128)(2,1)S(1)} %bitcast.105, bf16[32,2,1,64,128]{4,1,0,3,2:T(2,128)(2,1)S(1)} %bitcast.104), kind=kLoop, calls=%fused_computation.23 | loop fusion | flops 1048576 | bytes 4194304 | tf_op jit(solution)/shard_map/transpose | solution.py:104
  36.7 4.2 %all-to-all-start.1 = ((bf16[32,2,2,64,128]{4,2,3,1,0:T(2,128)(2,1)}), bf16[32,2,2,64,128]{4,2,3,1,0:T(2,128)(2,1)S(1)}, u32[]{:S(2)}, u32[]{:S(2)}) async-start(bf16[32,2,2,64,128]{4,2,3,1,0:T(2,128)(2,1)} %copy_bitcast_fusion), calls=%async_computation.1 | async-start | bytes 4194304 | tf_op jit(solution)/shard_map/all_to_all | solution.py:105
  40.9 0.1 fusion.50
  41.1 1.3 gather_fusion
  42.5 1.3 gather_fusion.2
  43.8 1.3 gather_fusion.1
  45.1 1.3 gather_fusion.3
  46.4 0.1 select_bitcast_fusion.1
  46.5 0.1 broadcast_select_fusion.1
  46.6 0.1 multiply_subtract_fusion.1
  46.7 0.0 copy-start.9
  46.7 21.7 %all-to-all-done.1 = bf16[32,2,2,64,128]{4,2,3,1,0:T(2,128)(2,1)S(1)} async-done(((bf16[32,2,2,64,128]{4,2,3,1,0:T(2,128)(2,1)}), bf16[32,2,2,64,128]{4,2,3,1,0:T(2,128)(2,1)S(1)}, u32[]{:S(2)}, u32[]{:S(2)}) %all-to-all-start.1) | async-done | bytes 2097184 | tf_op jit(solution)/shard_map/all_to_all | solution.py:105
  68.4 2.2 %copy.60 = bf16[32,2,2,64,128]{4,1,0,3,2:T(2,128)(2,1)S(1)} copy(bf16[32,2,2,64,128]{4,2,3,1,0:T(2,128)(2,1)S(1)} %all-to-all-done.1) | data formatting | bytes 4194304 | tf_op jit(solution)/shard_map/all_to_all | solution.py:105
  70.6 0.0 copy-start.4
  70.6 0.0 copy-start.5
  70.6 1.2 fusion.74
  71.9 0.6 multiply_add_fusion
  72.5 0.0 copy-start.3
  72.5 0.4 pad_maximum_fusion
  72.9 0.5 copy-done.3
  73.4 3.9 %fusion.8 = f32[32,2,64,256]{3,2,1,0:T(8,128)S(1)} fusion(f32[256,256,1,1]{1,0,3,2:T(8,128)S(1)} %copy-done.3, f32[32,2,64,256]{3,0,2,1:T(8,128)S(1)} %pad_maximum_fusion), kind=kOutput, calls=%fused_computation.15 | convolution fusion | flops 1610612736 | bytes 8650752 | tf_op jit(solution)/shard_map/...b,bm->...m/dot_general | solution.py:50
  77.4 4.1 %fusion.3 = f32[32,2,64,256]{3,0,2,1:T(8,128)S(1)} fusion(f32[64,64,256]{2,1,0:T(8,128)S(1)} %bitcast.100, pred[32,2,64,1]{2,1,0,3:T(4,128)(4,1)S(1)} %bitcast.107), kind=kOutput, calls=%fused_computation.10 | convolution fusion | flops 402653184 | bytes 8392704 | tf_op jit(solution)/shard_map/uv,vcb->ucb/dot_general | solution.py:138
  81.5 3.9 %fusion.5 = f32[32,2,64,256]{3,2,1,0:T(8,128)S(1)} fusion(f32[32,2,64,256]{3,0,2,1:T(8,128)S(1)} %fusion.3, f32[128,128]{1,0:T(8,128)S(1)} %fusion.46), kind=kOutput, calls=%fused_computation.12 | convolution fusion | flops 1610940416 | bytes 8454144 | tf_op jit(solution)/shard_map/...b,bm->...m/dot_general | solution.py:141
  85.4 0.2 fusion.23
  85.6 1.2 add_multiply_fusion.1
  86.8 0.0 copy-start.2
  86.8 1.1 add_subtract_fusion
  87.9 1.0 fusion.10
  88.9 0.3 subtract_bitcast_fusion
  89.3 0.0 copy-start.8
  89.3 0.3 pad_maximum_fusion.2
  89.6 0.4 copy-done.8
  90.0 2.2 %fusion.18 = f32[64,2,32,128]{3,0,2,1:T(8,128)S(1)} fusion(f32[64,64,1,1]{1,0,3,2:T(8,128)S(1)} %copy-done.8, f32[64,2,32,128]{3,2,1,0:T(8,128)S(1)} %bitcast.102), kind=kOutput, calls=%fused_computation.32 | convolution fusion | flops 201326592 | bytes 4210688 | tf_op jit(solution)/shard_map/qk,k...->q.../dot_general | solution.py:46
  92.2 0.3 fusion.26
  92.5 0.1 pad_maximum_fusion.3
  92.6 0.4 copy.66
  93.0 0.0 copy-start.10
  93.0 23.7 %all_to_all.20 = bf16[32,2,2,32,128]{4,3,1,2,0:T(8,128)(2,1)S(1)} all-to-all(bf16[32,2,2,32,128]{4,3,1,2,0:T(8,128)(2,1)S(1)} %copy.66), channel_id=1, replica_groups=mesh['seq'=32,'tp'=4] {'seq'}, dimensions={0} | all-to-all | bytes 2097152 | tf_op jit(solution)/shard_map/all_to_all | solution.py:190
  116.8 0.1 copy.67
  116.9 0.0 copy-start.1
  116.9 0.7 fusion.21
  117.6 0.3 copy.69
  118.0 14.1 %all_to_all.21 = bf16[32,64,128]{2,1,0:T(8,128)(2,1)S(1)} all-to-all(bf16[32,64,128]{2,1,0:T(8,128)(2,1)S(1)} %bitcast.106), channel_id=1, replica_groups=mesh['seq'=32,'tp'=4] {'seq'}, dimensions={0} | all-to-all | bytes 1048576 | tf_op jit(solution)/shard_map/all_to_all | solution.py:196
  132.0 0.1 fusion.24
  132.1 2.7 %collective-permute-start = (bf16[64,4096]{1,0:T(8,128)(2,1)S(1)}, bf16[64,4096]{1,0:T(8,128)(2,1)S(1)}, u32[]{:S(2)}, u32[]{:S(2)}) collective-permute-start(bf16[64,4096]{1,0:T(8,128)(2,1)S(1)} %fusion.24), channel_id=1, source_target_pairs={{0,2},{1,3},{2,0},{3,1},{4,6},{5,7},{6,4},{7,5},{8,10},{9,11},{10,... | collective-permute-start | bytes 1572872 | tf_op jit(solution)/shard_map/ppermute | solution.py:205
  134.8 0.4 fusion.58
  135.2 9.3 %collective-permute-done = bf16[64,4096]{1,0:T(8,128)(2,1)S(1)} collective-permute-done((bf16[64,4096]{1,0:T(8,128)(2,1)S(1)}, bf16[64,4096]{1,0:T(8,128)(2,1)S(1)}, u32[]{:S(2)}, u32[]{:S(2)}) %collective-permute-start) | collective-permute-done | bytes 524320 | tf_op jit(solution)/shard_map/ppermute | solution.py:205
  144.5 0.3 fusion.2
  144.8 3.7 %collective-permute-start.1 = (bf16[64,4096]{1,0:T(8,128)(2,1)S(1)}, bf16[64,4096]{1,0:T(8,128)(2,1)S(1)}, u32[]{:S(2)}, u32[]{:S(2)}) collective-permute-start(bf16[64,4096]{1,0:T(8,128)(2,1)S(1)} %fusion.2), channel_id=1, source_target_pairs={{0,1},{1,0},{2,3},{3,2},{4,5},{5,4},{6,7},{7,6},{8,9},{9,8},{10,11... | collective-permute-start | bytes 1572872 | tf_op jit(solution)/shard_map/ppermute | solution.py:218
  148.5 0.3 fusion.61
  148.9 1.2 collective-permute-done.1
  150.1 1.2 fusion.1
  (26 shorter events, 0.1 us)
Async XLA Ops:
  0.0 134.8 %copy-start = (bf16[256,256]{1,0:T(8,128)(2,1)S(1)}, bf16[256,256]{1,0:T(8,128)(2,1)}, u32[]{:S(2)}) copy-start(bf16[256,256]{1,0:T(8,128)(2,1)} %param.32) | copy-start | bytes 393220
  0.0 13.3 %copy-start.11 = (f32[64,128]{1,0:T(8,128)S(1)}, f32[64,128]{1,0:T(8,128)}, u32[]{:S(2)}) copy-start(f32[64,128]{1,0:T(8,128)} %constant.174.clone) | copy-start | bytes 98308
  0.0 13.3 %copy-start.12 = (f32[64,128]{1,0:T(8,128)S(1)}, f32[64,128]{1,0:T(8,128)}, u32[]{:S(2)}) copy-start(f32[64,128]{1,0:T(8,128)} %constant.175.clone) | copy-start | bytes 98308
  2.7 26.6 %copy-start.7 = (f32[64,32,1]{0,1,2:T(8,128)S(1)}, f32[64,32,1]{0,1,2:T(8,128)}, u32[]{:S(2)}) copy-start(f32[64,32,1]{0,1,2:T(8,128)} %constant.204) | copy-start | bytes 24580
  2.7 26.5 %all-to-all-start = ((bf16[32,128,128]{2,1,0:T(8,128)(2,1)}), bf16[32,128,128]{2,1,0:T(8,128)(2,1)S(1)}, u32[]{:S(2)}, u32[]{:S(2)}) async-start(bf16[32,128,128]{2,1,0:T(8,128)(2,1)} %shard_map.208), calls=%async_computation | async-start | bytes 2097152 | tf_op jit(solution)/shard_map/all_to_all | solution.py:87
  29.3 1.6 %copy-start.6 = (f32[64,32,1]{0,1,2:T(8,128)S(1)}, f32[64,32,1]{0,1,2:T(8,128)}, u32[]{:S(2)}) copy-start(f32[64,32,1]{0,1,2:T(8,128)} %constant.205) | copy-start | bytes 24580
  36.7 31.7 %all-to-all-start.1 = ((bf16[32,2,2,64,128]{4,2,3,1,0:T(2,128)(2,1)}), bf16[32,2,2,64,128]{4,2,3,1,0:T(2,128)(2,1)S(1)}, u32[]{:S(2)}, u32[]{:S(2)}) async-start(bf16[32,2,2,64,128]{4,2,3,1,0:T(2,128)(2,1)} %copy_bitcast_fusion), calls=%async_computation.1 | async-start | bytes 4194304 | tf_op jit(solution)/shard_map/all_to_all | solution.py:105
  46.7 23.9 %copy-start.9 = (f32[64,64,1,1]{1,0,3,2:T(8,128)S(1)}, f32[64,64,1,1]{1,0,3,2:T(8,128)}, u32[]{:S(2)}) copy-start(f32[64,64,1,1]{1,0,3,2:T(8,128)} %constant.203) | copy-start | bytes 49156
  70.6 1.3 copy-start.4
  70.6 1.3 copy-start.5
  72.5 1.0 copy-start.3
  86.8 1.1 copy-start.2
  89.3 0.8 copy-start.8
  93.0 23.9 %copy-start.10 = (f32[64,128,1]{1,0,2:T(8,128)S(1)}, f32[64,128,1]{1,0,2:T(8,128)}, u32[]{:S(2)}) copy-start(f32[64,128,1]{1,0,2:T(8,128)} %constant.208) | copy-start | bytes 98308
  116.9 15.1 %copy-start.1 = (bf16[64,4096]{1,0:T(8,128)(2,1)S(1)}, bf16[64,4096]{1,0:T(8,128)(2,1)}, u32[]{:S(2)}) copy-start(bf16[64,4096]{1,0:T(8,128)(2,1)} %param.28) | copy-start | bytes 1572868
  132.1 12.3 %collective-permute-start = (bf16[64,4096]{1,0:T(8,128)(2,1)S(1)}, bf16[64,4096]{1,0:T(8,128)(2,1)S(1)}, u32[]{:S(2)}, u32[]{:S(2)}) collective-permute-start(bf16[64,4096]{1,0:T(8,128)(2,1)S(1)} %fusion.24), channel_id=1, source_target_pairs={{0,2},{1,3},{2,0},{3,1},{4,6},{5,7},{6,4},{7,5},{8,10},{9,11},{10,... | collective-permute-start | bytes 1572872 | tf_op jit(solution)/shard_map/ppermute | solution.py:205
  144.8 5.2 %collective-permute-start.1 = (bf16[64,4096]{1,0:T(8,128)(2,1)S(1)}, bf16[64,4096]{1,0:T(8,128)(2,1)S(1)}, u32[]{:S(2)}, u32[]{:S(2)}) collective-permute-start(bf16[64,4096]{1,0:T(8,128)(2,1)S(1)} %fusion.2), channel_id=1, source_target_pairs={{0,1},{1,0},{2,3},{3,2},{4,5},{5,4},{6,7},{7,6},{8,9},{9,8},{10,11... | collective-permute-start | bytes 1572872 | tf_op jit(solution)/shard_map/ppermute | solution.py:218

commit v6 on v5

--- a/solution.py
+++ b/solution.py
@@ -186,12 +186,14 @@
     sin_b = (sin_blk[:, :, None] * cos_off[None] + cos_blk[:, :, None] * sin_off[None])[:, :, None, :]
     reverted_real = back_real * cos_b - back_imag * sin_b
     reverted_imag = back_imag * cos_b + back_real * sin_b
-    reverted = jnp.stack([reverted_real, reverted_imag], axis=2).astype(bf16)
+    reverted = jnp.stack([reverted_real, reverted_imag], axis=1).astype(bf16)
     moved = lax.all_to_all(reverted, "seq", 0, 0, tiled=True).astype(f32)
     moved = moved.reshape(2 * rows, pairs, width)
 
     cl_np, sl_np = np_turns(np.arange(seqs), row_ids, rows)
-    merged = major(block_table(cl_np, sl_np, 1.0, True, rows_reim_inner=True), moved)
+    last_tab = block_table(cl_np, sl_np, 1.0, True, rows_reim_inner=True).reshape(2 * seqs, seqs, 2, 2)
+    last_tab = last_tab.transpose(0, 1, 3, 2).reshape(2 * seqs, 2 * rows)
+    merged = major(last_tab, moved)
     merged = merged.reshape(seqs, chans, width) * (1.0 / full)
     arrived = lax.all_to_all(merged.astype(bf16), "seq", 0, 0, tiled=True)
     conv = arrived.astype(f32).transpose(1, 0, 2).reshape(chans, length)

time: 152 us -> 152 us (level)
  no operation moved by 1% of the time
where the time goes in v6:
time: 152 us; the launch traced here: 151 us
  waiting for transfers between devices  48.1 us (32%)
  blocking collectives  37.8 us (25%)
  matrix products  23.6 us (16%)
  starting transfers between devices  20.3 us (13%)
  local copies, waits for them, and re-layouts  9.99 us (7%)
  other arithmetic  8.34 us (5%)
  Pallas kernels  2.7 us (2%)
    all_to_all x1, blocking collectives, body(): moved = lax.all_to_all(reverted, 'seq', 0, 0, tiled=True).astype(f32)  23.7 us
    all_to_all x1, waiting for transfers between devices, body(): recv = lax.all_to_all(spread, 'seq', 0, 0, tiled=True).astype(f32)  21.7 us
    all_to_all x1, waiting for transfers between devices, body(): got = lax.all_to_all(send, 'seq', 0, 0, tiled=True).astype(f32)  15.9 us
    all_to_all x1, blocking collectives, body(): arrived = lax.all_to_all(merged.astype(bf16), 'seq', 0, 0, tiled=True)  14.1 us
    all_to_all x1, starting transfers between devices, body(): got = lax.all_to_all(send, 'seq', 0, 0, tiled=True).astype(f32)  9.84 us
    ppermute x1, waiting for transfers between devices, body(): gated_far = lax.ppermute(gated_out, 'tp', cross)  9.34 us
    dot_general x7, matrix products, major(): return jnp.einsum('qk,k...->q...', table, data, precision=HIGH)  8.29 us
    dot_general x2, matrix products, minor(): return jnp.einsum('...b,bm->...m', data, table, precision=HIGH)  4.94 us
  transfers between devices with their start and end apart: 4, of which 4 were waited for; matrix products, arithmetic and copies ran while one was open for 5% of the time, Pallas kernels for 0%

profile of v6, /device:TPU:1, one launch (start us, length us, event | category | flops | bytes accessed | tf_op | source)
XLA Modules:
  0.0 151.3 jit_solution(869527681430170614)
XLA Ops:
  0.0 0.0 copy-start
  0.0 2.7 %shard_map.208 = bf16[32,128,128]{2,1,0:T(8,128)(2,1)} custom-call(bf16[64,4096]{1,0:T(8,128)(2,1)} %key_ref.1, bf16[64,4096]{1,0:T(8,128)(2,1)} %value_ref.1, f32[64,4096]{1,0:T(8,128)} %taps_ref.1), custom_call_target="tpu_custom_call" | custom-call | tf_op jit(solution)/shard_map/pallas_call | solution.py:69
  2.7 9.8 %all-to-all-start = ((bf16[32,128,128]{2,1,0:T(8,128)(2,1)}), bf16[32,128,128]{2,1,0:T(8,128)(2,1)S(1)}, u32[]{:S(2)}, u32[]{:S(2)}) async-start(bf16[32,128,128]{2,1,0:T(8,128)(2,1)} %shard_map.208), calls=%async_computation | async-start | bytes 2097152 | tf_op jit(solution)/shard_map/all_to_all | solution.py:87
  12.6 0.7 fusion.64
  13.3 0.0 copy-done.11
  13.3 0.1 multiply_subtract_fusion.2
  13.4 15.9 %all-to-all-done = bf16[32,128,128]{2,1,0:T(8,128)(2,1)S(1)} async-done(((bf16[32,128,128]{2,1,0:T(8,128)(2,1)}), bf16[32,128,128]{2,1,0:T(8,128)(2,1)S(1)}, u32[]{:S(2)}, u32[]{:S(2)}) %all-to-all-start) | async-done | bytes 1048608 | tf_op jit(solution)/shard_map/all_to_all | solution.py:87
  29.3 0.1 fusion.74
  29.3 0.0 copy-start.6
  29.4 0.8 fusion.33
  30.1 0.8 fusion.29
  30.9 0.9 convolution_add_fusion.2
  31.9 1.4 fusion.15
  33.3 3.4 %copy_bitcast_fusion = bf16[32,2,2,64,128]{4,2,3,1,0:T(2,128)(2,1)} fusion(bf16[32,2,1,64,128]{4,1,0,3,2:T(2,128)(2,1)S(1)} %bitcast.113, bf16[32,2,1,64,128]{4,1,0,3,2:T(2,128)(2,1)S(1)} %bitcast.112), kind=kLoop, calls=%fused_computation.23 | loop fusion | flops 1048576 | bytes 4194304 | tf_op jit(solution)/shard_map/transpose | solution.py:104
  36.7 4.2 %all-to-all-start.1 = ((bf16[32,2,2,64,128]{4,2,3,1,0:T(2,128)(2,1)}), bf16[32,2,2,64,128]{4,2,3,1,0:T(2,128)(2,1)S(1)}, u32[]{:S(2)}, u32[]{:S(2)}) async-start(bf16[32,2,2,64,128]{4,2,3,1,0:T(2,128)(2,1)} %copy_bitcast_fusion), calls=%async_computation.1 | async-start | bytes 4194304 | tf_op jit(solution)/shard_map/all_to_all | solution.py:105
  40.9 0.1 fusion.51
  41.1 1.3 gather_fusion
  42.5 1.3 gather_fusion.2
  43.8 1.3 gather_fusion.1
  45.1 1.3 gather_fusion.3
  46.4 0.1 select_bitcast_fusion.1
  46.5 0.1 broadcast_select_fusion.1
  46.6 0.1 multiply_subtract_fusion.1
  46.7 0.0 copy-start.10
  46.7 21.7 %all-to-all-done.1 = bf16[32,2,2,64,128]{4,2,3,1,0:T(2,128)(2,1)S(1)} async-done(((bf16[32,2,2,64,128]{4,2,3,1,0:T(2,128)(2,1)}), bf16[32,2,2,64,128]{4,2,3,1,0:T(2,128)(2,1)S(1)}, u32[]{:S(2)}, u32[]{:S(2)}) %all-to-all-start.1) | async-done | bytes 2097184 | tf_op jit(solution)/shard_map/all_to_all | solution.py:105
  68.4 2.2 %copy.58 = bf16[32,2,2,64,128]{4,1,0,3,2:T(2,128)(2,1)S(1)} copy(bf16[32,2,2,64,128]{4,2,3,1,0:T(2,128)(2,1)S(1)} %all-to-all-done.1) | data formatting | bytes 4194304 | tf_op jit(solution)/shard_map/all_to_all | solution.py:105
  70.6 0.0 copy-start.4
  70.6 0.0 copy-start.5
  70.6 1.2 fusion.75
  71.8 0.0 copy-done.4
  71.9 0.6 multiply_add_fusion
  72.5 0.0 copy-start.3
  72.5 0.4 pad_maximum_fusion
  72.9 0.5 copy-done.3
  73.4 3.9 %fusion.8 = f32[32,2,64,256]{3,2,1,0:T(8,128)S(1)} fusion(f32[256,256,1,1]{1,0,3,2:T(8,128)S(1)} %copy-done.3, f32[32,2,64,256]{3,0,2,1:T(8,128)S(1)} %pad_maximum_fusion), kind=kOutput, calls=%fused_computation.15 | convolution fusion | flops 1610612736 | bytes 8650752 | tf_op jit(solution)/shard_map/...b,bm->...m/dot_general | solution.py:50
  77.4 4.1 %fusion.3 = f32[32,2,64,256]{3,0,2,1:T(8,128)S(1)} fusion(f32[64,64,256]{2,1,0:T(8,128)S(1)} %bitcast.109, pred[32,2,64,1]{2,1,0,3:T(4,128)(4,1)S(1)} %bitcast.115), kind=kOutput, calls=%fused_computation.10 | convolution fusion | flops 402653184 | bytes 8392704 | tf_op jit(solution)/shard_map/uv,vcb->ucb/dot_general | solution.py:138
  81.5 3.9 %fusion.5 = f32[32,2,64,256]{3,2,1,0:T(8,128)S(1)} fusion(f32[32,2,64,256]{3,0,2,1:T(8,128)S(1)} %fusion.3, f32[128,128]{1,0:T(8,128)S(1)} %fusion.47), kind=kOutput, calls=%fused_computation.12 | convolution fusion | flops 1610940416 | bytes 8454144 | tf_op jit(solution)/shard_map/...b,bm->...m/dot_general | solution.py:141
  85.4 0.2 fusion.24
  85.6 1.2 add_multiply_fusion.1
  86.8 0.0 copy-start.2
  86.8 1.1 add_subtract_fusion
  87.9 1.0 fusion.10
  88.9 0.3 subtract_bitcast_fusion
  89.3 0.0 copy-start.9
  89.3 0.3 pad_maximum_fusion.2
  89.6 0.4 copy-done.9
  90.0 2.2 %fusion.18 = f32[64,2,32,128]{3,0,2,1:T(8,128)S(1)} fusion(f32[64,64,1,1]{1,0,3,2:T(8,128)S(1)} %copy-done.9, f32[64,2,32,128]{3,2,1,0:T(8,128)S(1)} %bitcast.111), kind=kOutput, calls=%fused_computation.32 | convolution fusion | flops 201326592 | bytes 4210688 | tf_op jit(solution)/shard_map/qk,k...->q.../dot_general | solution.py:46
  92.2 0.3 fusion.27
  92.5 0.1 pad_maximum_fusion.3
  92.6 0.0 copy-start.8
  92.6 0.4 copy.64
  93.0 23.7 %all_to_all.20 = bf16[32,2,2,32,128]{4,3,2,1,0:T(8,128)(2,1)S(1)} all-to-all(bf16[32,2,2,32,128]{4,3,2,1,0:T(8,128)(2,1)S(1)} %copy.64), channel_id=1, replica_groups=mesh['seq'=32,'tp'=4] {'seq'}, dimensions={0} | all-to-all | bytes 2097152 | tf_op jit(solution)/shard_map/all_to_all | solution.py:190
  116.8 1.0 fusion.22
  117.7 0.3 copy.66
  118.1 14.1 %all_to_all.21 = bf16[32,64,128]{2,1,0:T(8,128)(2,1)S(1)} all-to-all(bf16[32,64,128]{2,1,0:T(8,128)(2,1)S(1)} %bitcast.114), channel_id=1, replica_groups=mesh['seq'=32,'tp'=4] {'seq'}, dimensions={0} | all-to-all | bytes 1048576 | tf_op jit(solution)/shard_map/all_to_all | solution.py:198
  132.2 0.1 fusion.25
  132.3 2.7 %collective-permute-start = (bf16[64,4096]{1,0:T(8,128)(2,1)S(1)}, bf16[64,4096]{1,0:T(8,128)(2,1)S(1)}, u32[]{:S(2)}, u32[]{:S(2)}) collective-permute-start(bf16[64,4096]{1,0:T(8,128)(2,1)S(1)} %fusion.25), channel_id=1, source_target_pairs={{0,2},{1,3},{2,0},{3,1},{4,6},{5,7},{6,4},{7,5},{8,10},{9,11},{10,... | collective-permute-start | bytes 1572872 | tf_op jit(solution)/shard_map/ppermute | solution.py:207
  134.9 0.3 fusion.59
  135.3 9.3 %collective-permute-done = bf16[64,4096]{1,0:T(8,128)(2,1)S(1)} collective-permute-done((bf16[64,4096]{1,0:T(8,128)(2,1)S(1)}, bf16[64,4096]{1,0:T(8,128)(2,1)S(1)}, u32[]{:S(2)}, u32[]{:S(2)}) %collective-permute-start) | collective-permute-done | bytes 524320 | tf_op jit(solution)/shard_map/ppermute | solution.py:207
  144.6 0.4 fusion.2
  145.0 3.6 %collective-permute-start.1 = (bf16[64,4096]{1,0:T(8,128)(2,1)S(1)}, bf16[64,4096]{1,0:T(8,128)(2,1)S(1)}, u32[]{:S(2)}, u32[]{:S(2)}) collective-permute-start(bf16[64,4096]{1,0:T(8,128)(2,1)S(1)} %fusion.2), channel_id=1, source_target_pairs={{0,1},{1,0},{2,3},{3,2},{4,5},{5,4},{6,7},{7,6},{8,9},{9,8},{10,11... | collective-permute-start | bytes 1572872 | tf_op jit(solution)/shard_map/ppermute | solution.py:220
  148.6 0.3 fusion.62
  149.0 1.2 collective-permute-done.1
  150.2 1.1 fusion.1
  (25 shorter events, 0.1 us)
Async XLA Ops:
  0.0 134.9 %copy-start = (bf16[256,256]{1,0:T(8,128)(2,1)S(1)}, bf16[256,256]{1,0:T(8,128)(2,1)}, u32[]{:S(2)}) copy-start(bf16[256,256]{1,0:T(8,128)(2,1)} %param.32) | copy-start | bytes 393220
  0.0 13.3 %copy-start.11 = (f32[64,128]{1,0:T(8,128)S(1)}, f32[64,128]{1,0:T(8,128)}, u32[]{:S(2)}) copy-start(f32[64,128]{1,0:T(8,128)} %constant.174.clone) | copy-start | bytes 98308
  0.0 13.3 %copy-start.12 = (f32[64,128]{1,0:T(8,128)S(1)}, f32[64,128]{1,0:T(8,128)}, u32[]{:S(2)}) copy-start(f32[64,128]{1,0:T(8,128)} %constant.175.clone) | copy-start | bytes 98308
  2.7 26.6 %copy-start.7 = (f32[64,32,1]{0,1,2:T(8,128)S(1)}, f32[64,32,1]{0,1,2:T(8,128)}, u32[]{:S(2)}) copy-start(f32[64,32,1]{0,1,2:T(8,128)} %constant.206) | copy-start | bytes 24580
  2.7 26.5 %all-to-all-start = ((bf16[32,128,128]{2,1,0:T(8,128)(2,1)}), bf16[32,128,128]{2,1,0:T(8,128)(2,1)S(1)}, u32[]{:S(2)}, u32[]{:S(2)}) async-start(bf16[32,128,128]{2,1,0:T(8,128)(2,1)} %shard_map.208), calls=%async_computation | async-start | bytes 2097152 | tf_op jit(solution)/shard_map/all_to_all | solution.py:87
  29.3 1.6 %copy-start.6 = (f32[64,32,1]{0,1,2:T(8,128)S(1)}, f32[64,32,1]{0,1,2:T(8,128)}, u32[]{:S(2)}) copy-start(f32[64,32,1]{0,1,2:T(8,128)} %constant.207) | copy-start | bytes 24580
  36.7 31.7 %all-to-all-start.1 = ((bf16[32,2,2,64,128]{4,2,3,1,0:T(2,128)(2,1)}), bf16[32,2,2,64,128]{4,2,3,1,0:T(2,128)(2,1)S(1)}, u32[]{:S(2)}, u32[]{:S(2)}) async-start(bf16[32,2,2,64,128]{4,2,3,1,0:T(2,128)(2,1)} %copy_bitcast_fusion), calls=%async_computation.1 | async-start | bytes 4194304 | tf_op jit(solution)/shard_map/all_to_all | solution.py:105
  46.7 23.9 %copy-start.10 = (f32[64,64,1,1]{1,0,3,2:T(8,128)S(1)}, f32[64,64,1,1]{1,0,3,2:T(8,128)}, u32[]{:S(2)}) copy-start(f32[64,64,1,1]{1,0,3,2:T(8,128)} %constant.205) | copy-start | bytes 49156
  70.6 1.3 copy-start.4
  70.6 1.3 copy-start.5
  72.5 1.0 copy-start.3
  86.8 1.1 copy-start.2
  89.3 0.8 copy-start.9
  92.6 24.2 %copy-start.8 = (f32[64,32,2,2,1]{0,1,3,2,4:T(8,128)S(1)}, f32[64,32,2,2,1]{0,1,3,2,4:T(8,128)}, u32[]{:S(2)}) copy-start(f32[64,32,2,2,1]{0,1,3,2,4:T(8,128)} %constant.210) | copy-start | bytes 98308
  116.8 15.4 %copy-start.1 = (bf16[64,4096]{1,0:T(8,128)(2,1)S(1)}, bf16[64,4096]{1,0:T(8,128)(2,1)}, u32[]{:S(2)}) copy-start(bf16[64,4096]{1,0:T(8,128)(2,1)} %param.28) | copy-start | bytes 1572868
  132.3 12.3 %collective-permute-start = (bf16[64,4096]{1,0:T(8,128)(2,1)S(1)}, bf16[64,4096]{1,0:T(8,128)(2,1)S(1)}, u32[]{:S(2)}, u32[]{:S(2)}) collective-permute-start(bf16[64,4096]{1,0:T(8,128)(2,1)S(1)} %fusion.25), channel_id=1, source_target_pairs={{0,2},{1,3},{2,0},{3,1},{4,6},{5,7},{6,4},{7,5},{8,10},{9,11},{10,... | collective-permute-start | bytes 1572872 | tf_op jit(solution)/shard_map/ppermute | solution.py:207
  145.0 5.2 %collective-permute-start.1 = (bf16[64,4096]{1,0:T(8,128)(2,1)S(1)}, bf16[64,4096]{1,0:T(8,128)(2,1)S(1)}, u32[]{:S(2)}, u32[]{:S(2)}) collective-permute-start(bf16[64,4096]{1,0:T(8,128)(2,1)S(1)} %fusion.2), channel_id=1, source_target_pairs={{0,1},{1,0},{2,3},{3,2},{4,5},{5,4},{6,7},{7,6},{8,9},{9,8},{10,11... | collective-permute-start | bytes 1572872 | tf_op jit(solution)/shard_map/ppermute | solution.py:220
